TPU v7x, 32 devices: a whole 2x2x4 slice. The times are simulated.
32 devices in a mesh: dp: 4 (over z), seq: 2 (over y), expert: 4 (over x, core).
Axes of the slice: x: 2, y: 2, z: 4, core: 2. Of those that a mesh axis runs over, the one named last changes fastest.
Arguments:
- out_grad: bfloat16 [4096, 1024], P(('dp', 'seq', 'expert')), may hold values from -6 to 6
- routes: int32 [4096, 2], P(('dp', 'seq', 'expert')), may hold values from 0 to 3, all different within a row; in each aligned block of 128 rows (0 to 127, 128 to 255, ...) at most 72 rows name the same one
- gates: bfloat16 [4096, 2], P(('dp', 'seq', 'expert')), may hold values from 0.099609375 to 0.8984375
- saved_input: bfloat16 [4, 4, 4, 2, 72, 1024], P('dp', 'expert'), may hold values from -6 to 6
- saved_preact: bfloat16 [4, 4, 4, 2, 72, 2048], P('dp', 'expert', None, None, None, 'seq'), may hold values from -6 to 6
- w_in: bfloat16 [4, 1024, 2048], P('expert', None, 'seq'), may hold values from -0.1875 to 0.1875
- w_out: bfloat16 [4, 2048, 1024], P('expert', 'seq'), may hold values from -0.125 to 0.125
Outputs:
- input_grad: bfloat16 [4096, 1024], P(('dp', 'seq', 'expert'))
- gate_grad: bfloat16 [4096, 2], P(('dp', 'seq', 'expert'))
- weight_grad: float32 [4, 1024, 2048], P('expert', 'dp', 'seq')
Inputs may be any that keep to these rules, and one draw needn't show every extreme that they name: `routes`: the two experts of a token differ; within the 128 tokens of one device no expert is chosen more than 72 times, a bound that some block reaches.
All inputs are finite; a program needn't handle non-finite values.
Results may differ from a plain program's by a relative error of at most 0.0058.
Values may be sent and summed in bfloat16 or wider, within the bound.
No kernel may reach another device: no remote copies, remote signals or barrier semaphores. Data moves between devices by JAX's collectives and lax.ppermute only.
A program may use at most 64 MiB of HBM per device.

v0:
```python
import jax
import jax.numpy as jnp
from jax import lax
from jax.sharding import PartitionSpec as P


def slot_targets(block_routes, experts, capacity):
    flat_routes = block_routes.reshape(-1)
    one_hot = (flat_routes[:, None] == jnp.arange(experts, dtype=jnp.int32)[None, :]).astype(
        jnp.int32
    )
    before = jnp.cumsum(one_hot, axis=0) - one_hot
    slot_rank = jnp.sum(before * one_hot, axis=1)
    return (flat_routes * capacity + slot_rank).reshape(block_routes.shape)


def silu_parts(preact):
    sigma = jax.nn.sigmoid(preact)
    return (preact * sigma, sigma * (1.0 + preact * (1.0 - sigma)))


def on_device(out_grad, routes, gates, saved_input, saved_preact, w_in, w_out):
    model_width = out_grad.shape[1]
    experts = lax.axis_size("expert")
    halves = lax.axis_size("seq")
    data_groups = lax.axis_size("dp")
    capacity = saved_input.shape[4]
    cell_ids = jnp.arange(experts * capacity, dtype=jnp.int32)
    targets = slot_targets(routes, experts, capacity)
    first_pick = targets[:, 0][None, :] == cell_ids[:, None]
    second = targets[:, 1][None, :] == cell_ids[:, None]
    send_matrix = (first_pick | second).astype(jnp.bfloat16)
    send_rows = jnp.dot(send_matrix, out_grad, preferred_element_type=jnp.float32)
    send_rows = send_rows.astype(jnp.bfloat16).reshape(experts, capacity, model_width)
    gate_cells = jnp.sum(
        jnp.where(first_pick, gates[:, 0][None, :].astype(jnp.float32), 0.0)
        + jnp.where(second, gates[:, 1][None, :].astype(jnp.float32), 0.0),
        axis=1,
    )
    gate_cells = gate_cells.astype(jnp.bfloat16).reshape(experts, capacity)
    group_rows, group_gates = (
        lax.all_gather(send_rows, "seq", axis=1, tiled=True),
        lax.all_gather(gate_cells, "seq", axis=1, tiled=True),
    )
    row_block, row_gates = (
        lax.all_to_all(group_rows, "expert", split_axis=0, concat_axis=0, tiled=True),
        lax.all_to_all(group_gates, "expert", split_axis=0, concat_axis=0, tiled=True),
    )
    row_count = experts * halves * capacity
    flat_rows = row_block.reshape(row_count, model_width)
    flat_gates = row_gates.reshape(row_count, 1).astype(jnp.float32)
    input_rows = saved_input.reshape(row_count, model_width)
    preact_rows = saved_preact.reshape(row_count, -1).astype(jnp.float32)
    w_in_half = w_in[0]
    w_out_half = w_out[0]
    raw_grad = lax.dot_general(
        flat_rows, w_out_half, (((1,), (1,)), ((), ())), preferred_element_type=jnp.float32
    )
    activation, slope = silu_parts(preact_rows)
    gate_part = jnp.sum(activation * raw_grad, axis=1)
    delta_rows = (flat_gates * raw_grad * slope).astype(jnp.bfloat16)
    grad_part = lax.dot_general(
        delta_rows, w_in_half, (((1,), (1,)), ((), ())), preferred_element_type=jnp.float32
    )
    weight_share = lax.psum_scatter(
        lax.dot_general(
            input_rows, delta_rows, (((0,), (0,)), ((), ())), preferred_element_type=jnp.float32
        ),
        "dp",
        scatter_dimension=0,
        tiled=True,
    )
    weight_grad = (weight_share * (1.0 / data_groups))[None]
    summed_rows, summed_gates = (
        lax.psum_scatter(
            grad_part.reshape(experts, halves * capacity, model_width),
            "seq",
            scatter_dimension=1,
            tiled=True,
        ),
        lax.psum_scatter(
            gate_part.reshape(experts, halves * capacity), "seq", scatter_dimension=1, tiled=True
        ),
    )
    back_rows, back_gates = (
        lax.all_to_all(
            summed_rows.astype(jnp.bfloat16), "expert", split_axis=0, concat_axis=0, tiled=True
        ),
        lax.all_to_all(
            summed_gates.astype(jnp.bfloat16), "expert", split_axis=0, concat_axis=0, tiled=True
        ),
    )
    back_flat = back_rows.reshape(experts * capacity, model_width)
    input_grad = lax.dot_general(
        send_matrix, back_flat, (((0,), (0,)), ((), ())), preferred_element_type=jnp.float32
    ).astype(jnp.bfloat16)
    gate_values = back_gates.reshape(experts * capacity).astype(jnp.float32)
    gate_first = jnp.sum(jnp.where(first_pick, gate_values[:, None], 0.0), axis=0)
    gate_second = jnp.sum(jnp.where(second, gate_values[:, None], 0.0), axis=0)
    gate_grad = jnp.stack([gate_first, gate_second], axis=1).astype(jnp.bfloat16)
    return (input_grad, gate_grad, weight_grad)


def solution(mesh):
    return jax.shard_map(
        on_device,
        mesh=mesh,
        in_specs=(
            P(("dp", "seq", "expert"), None),
            P(("dp", "seq", "expert"), None),
            P(("dp", "seq", "expert"), None),
            P("dp", "expert", None, None, None, None),
            P("dp", "expert", None, None, None, "seq"),
            P("expert", None, "seq"),
            P("expert", "seq", None),
        ),
        out_specs=(
            P(("dp", "seq", "expert"), None),
            P(("dp", "seq", "expert"), None),
            P("expert", "dp", "seq"),
        ),
        check_vma=False,
    )
```

profile of v0, /device:TPU:0, one launch (start us, length us, event | category | flops | bytes accessed | tf_op | source)
XLA Modules:
  0.0 214.0 jit_solution(13751752746852215241)
XLA Ops:
  7.2 0.9 copy.48
  8.5 1.2 reduce-window.6
  10.3 0.7 multiply_add_fusion
  11.0 2.1 convolution_convert_fusion
  13.1 25.6 %all-gather.3.cloned.1.call-done = bf16[4,144,1024]{2,1,0:T(8,128)(2,1)} async-done(((bf16[4,72,1024]{2,1,0:T(8,128)(2,1)}), bf16[4,144,1024]{2,1,0:T(8,128)(2,1)}) %all-gather.3.cloned.1.call-update) | async-done | bytes 1179664 | tf_op jit(solution)/shard_map/all_gather | solution.py:42
  38.8 3.5 %all-to-all-start.1 = ((bf16[4,144,1024]{2,1,0:T(8,128)(2,1)}), bf16[4,144,1024]{2,1,0:T(8,128)(2,1)S(1)}, u32[]{:S(2)}, u32[]{:S(2)}) async-start(bf16[4,144,1024]{2,1,0:T(8,128)(2,1)} %all-gather.3.cloned.1.call-done), calls=%async_computation.1 | async-start | bytes 2359296 | tf_op jit(solution)/shard_map/all_to_all | solution.py:46
  43.5 14.6 %all-to-all-done.1 = bf16[4,144,1024]{2,1,0:T(8,128)(2,1)S(1)} async-done(((bf16[4,144,1024]{2,1,0:T(8,128)(2,1)}), bf16[4,144,1024]{2,1,0:T(8,128)(2,1)S(1)}, u32[]{:S(2)}, u32[]{:S(2)}) %all-to-all-start.1) | async-done | bytes 1179680 | tf_op jit(solution)/shard_map/all_to_all | solution.py:46
  58.1 4.2 %fusion.8 = (f32[576]{0:T(1024)S(1)}, f32[576,1024]{1,0:T(8,128)}) fusion(bf16[576,1024]{1,0:T(8,128)(2,1)} %bitcast.78, bf16[576,1024]{1,0:T(8,128)(2,1)S(1)} %bitcast.77, bf16[1,1024,1024]{2,1,0:T(8,128)(2,1)S(1)} %copy-done), kind=kOutput, calls=%fused_computation.11 | convolution fusion | flops 1212087808 | bytes 6818048 | tf_op jit(solution)/shard_map/dot_general | solution.py:56
  62.4 4.9 %all-reduce = bf16[4,144]{1,0:T(4,128)(2,1)S(1)} all-reduce(f32[4,144]{1,0:T(4,128)S(1)} %reshape.97), channel_id=3, replica_groups=mesh['dp'=4,'seq'=2,'expert'=4] {'seq'}, use_global_device_ids=true, to_apply=%region_6.7.clone | all-reduce | flops 576 | bytes 3456
  68.0 3.2 %all-to-all-start.3 = ((bf16[4,1,72]{2,1,0:T(2,128)(2,1)}), bf16[4,1,72]{2,1,0:T(2,128)(2,1)S(1)}, u32[]{:S(2)}, u32[]{:S(2)}) async-start(bf16[4,1,72]{2,1,0:T(2,128)(2,1)} %copy.55), calls=%async_computation.4 | async-start | bytes 4096 | tf_op jit(solution)/shard_map/all_to_all | solution.py:89
  71.3 3.6 %all-to-all-done.3 = bf16[4,1,72]{2,1,0:T(2,128)(2,1)S(1)} async-done(((bf16[4,1,72]{2,1,0:T(2,128)(2,1)}), bf16[4,1,72]{2,1,0:T(2,128)(2,1)S(1)}, u32[]{:S(2)}, u32[]{:S(2)}) %all-to-all-start.3) | async-done | bytes 608 | tf_op jit(solution)/shard_map/all_to_all | solution.py:89
  75.3 4.2 %all-gather = bf16[2,72,4]{1,2,0:T(4,128)(2,1)S(1)} all-gather(bf16[1,72,4]{1,2,0:T(4,128)(2,1)S(1)} %bitcast.82), channel_id=1, replica_groups=mesh['dp'=4,'seq'=2,'expert'=4] {'seq'}, dimensions={0}, use_global_device_ids=true | all-gather | bytes 1728 | tf_op jit(solution)/shard_map/all_gather | solution.py:43
  79.6 6.1 %all_to_all.28 = bf16[4,1,144]{2,1,0:T(2,128)(2,1)S(1)} all-to-all(bf16[4,1,144]{2,1,0:T(2,128)(2,1)S(1)} %copy.54), channel_id=1, replica_groups=mesh['dp'=4,'seq'=2,'expert'=4] {'expert'}, dimensions={0} | all-to-all | bytes 2304 | tf_op jit(solution)/shard_map/all_to_all | solution.py:47
  85.9 3.0 %fusion.6 = bf16[576,1024]{1,0:T(8,128)(2,1)S(1)} fusion(f32[576,1024]{1,0:T(8,128)} %get-tuple-element.29, f32[576]{0:T(1024)S(1)} %reshape.101, bf16[1,1,4,2,72,1024]{5,4,3,2,1,0:T(8,128)(2,1)} %param.11), kind=kLoop, calls=%fused_computation.9 | loop fusion | flops 6488064 | bytes 4720896 | tf_op jit(solution)/shard_map/convert_element_type | solution.py:61
  88.9 2.9 %fusion.9 = f32[4,144,1024]{2,1,0:T(8,128)} fusion(bf16[4,144,1024]{2,1,0:T(8,128)(2,1)S(1)} %bitcast.79, bf16[1,1024,1024]{2,1,0:T(8,128)(2,1)S(1)} %copy-done.2), kind=kOutput, calls=%fused_computation.13 | convolution fusion | flops 1207959552 | bytes 5636096 | tf_op jit(solution)/shard_map/dot_general | solution.py:62
  91.8 5.0 %convolution_bitcast_fusion = f32[1024,1024]{0,1:T(8,128)} fusion(bf16[576,1024]{1,0:T(8,128)(2,1)S(1)} %fusion.6, bf16[576,1024]{1,0:T(8,128)(2,1)} %bitcast.85), kind=kOutput, calls=%fused_computation.12 | convolution fusion | flops 1207959552 | bytes 6553600 | tf_op jit(solution)/shard_map/dot_general | solution.py:66
  96.9 28.9 %reduce-scatter.4.cloned.1.call-done = f32[4,72,1024]{2,1,0:T(8,128)} async-done(((f32[4,144,1024]{2,1,0:T(8,128)}), f32[4,72,1024]{2,1,0:T(8,128)}) %reduce-scatter.4.cloned.1.call-update) | async-done | bytes 1179664 | tf_op jit(solution)/shard_map/reduce_scatter | solution.py:75
  125.8 2.2 %convert_element_type.94 = bf16[4,72,1024]{2,1,0:T(8,128)(2,1)} convert(f32[4,72,1024]{2,1,0:T(8,128)} %reduce-scatter.4.cloned.1.call-done) | non-fusion elementwise | flops 294912 | bytes 1769472 | tf_op jit(solution)/shard_map/convert_element_type | solution.py:87
  128.0 3.5 %all-to-all-start.2 = ((bf16[4,72,1024]{2,1,0:T(8,128)(2,1)}), bf16[4,72,1024]{2,1,0:T(8,128)(2,1)S(1)}, u32[]{:S(2)}, u32[]{:S(2)}) async-start(bf16[4,72,1024]{2,1,0:T(8,128)(2,1)} %convert_element_type.94), calls=%async_computation.3 | async-start | bytes 1179648 | tf_op jit(solution)/shard_map/all_to_all | solution.py:86
  132.0 9.0 %all-to-all-done.2 = bf16[4,72,1024]{2,1,0:T(8,128)(2,1)S(1)} async-done(((bf16[4,72,1024]{2,1,0:T(8,128)(2,1)}), bf16[4,72,1024]{2,1,0:T(8,128)(2,1)S(1)}, u32[]{:S(2)}, u32[]{:S(2)}) %all-to-all-start.2) | async-done | bytes 589856 | tf_op jit(solution)/shard_map/all_to_all | solution.py:86
  141.0 1.1 convolution_convert_fusion.1
  142.0 62.9 %reduce-scatter.6.cloned.1.call-done = f32[256,1024]{0,1:T(8,128)} async-done(((f32[1024,1024]{0,1:T(8,128)}), f32[256,1024]{0,1:T(8,128)}) %reduce-scatter.6.cloned.1.call-update) | async-done | bytes 1048592 | tf_op jit(solution)/shard_map/reduce_scatter | solution.py:65
  204.9 1.3 multiply_bitcast_fusion
  206.2 1.3 copy.56
  (42 shorter events, 3.5 us)
Async XLA Ops:
  7.2 50.9 %copy-start = (bf16[1,1024,1024]{2,1,0:T(8,128)(2,1)S(1)}, bf16[1,1024,1024]{2,1,0:T(8,128)(2,1)}, u32[]{:S(2)}) copy-start(bf16[1,1024,1024]{2,1,0:T(8,128)(2,1)} %param.13) | copy-start | bytes 6291460
  7.2 35.1 %copy-start.3 = (u32[32]{0:T(128)S(1)}, u32[32]{0:T(128)}, u32[]{:S(2)}) copy-start(u32[32]{0:T(128)} %constant.20) | copy-start | bytes 388
  7.2 31.6 %all-gather.3.cloned.1.call-start = ((), (), s32[]{:S(2)}) async-start(), calls=%async_computation.6 | async-start | bytes 1769472 | tf_op jit(solution)/shard_map/all_gather | solution.py:42
  38.8 19.3 %all-to-all-start.1 = ((bf16[4,144,1024]{2,1,0:T(8,128)(2,1)}), bf16[4,144,1024]{2,1,0:T(8,128)(2,1)S(1)}, u32[]{:S(2)}, u32[]{:S(2)}) async-start(bf16[4,144,1024]{2,1,0:T(8,128)(2,1)} %all-gather.3.cloned.1.call-done), calls=%async_computation.1 | async-start | bytes 2359296 | tf_op jit(solution)/shard_map/all_to_all | solution.py:46
  58.1 13.2 %copy-start.1 = (bf16[128,2]{0,1:T(2,128)(2,1)S(1)}, bf16[128,2]{0,1:T(2,128)(2,1)}, u32[]{:S(2)}) copy-start(bf16[128,2]{0,1:T(2,128)(2,1)} %param.9) | copy-start | bytes 1540
  68.0 6.9 %all-to-all-start.3 = ((bf16[4,1,72]{2,1,0:T(2,128)(2,1)}), bf16[4,1,72]{2,1,0:T(2,128)(2,1)S(1)}, u32[]{:S(2)}, u32[]{:S(2)}) async-start(bf16[4,1,72]{2,1,0:T(2,128)(2,1)} %copy.55), calls=%async_computation.4 | async-start | bytes 4096 | tf_op jit(solution)/shard_map/all_to_all | solution.py:89
  71.2 54.6 %reduce-scatter.4.cloned.1.call-start = ((), (), s32[]{:S(2)}) async-start(), calls=%async_computation.7 | async-start | bytes 3538944 | tf_op jit(solution)/shard_map/reduce_scatter | solution.py:75
  85.9 3.0 %copy-start.2 = (bf16[1,1024,1024]{2,1,0:T(8,128)(2,1)S(1)}, bf16[1,1024,1024]{2,1,0:T(8,128)(2,1)}, u32[]{:S(2)}) copy-start(bf16[1,1024,1024]{2,1,0:T(8,128)(2,1)} %param.12) | copy-start | bytes 6291460
  91.8 113.1 %reduce-scatter.6.cloned.1.call-start = ((), (), s32[]{:S(2)}) async-start(), calls=%async_computation.8 | async-start | bytes 5242880 | tf_op jit(solution)/shard_map/reduce_scatter | solution.py:65
  128.0 13.0 %all-to-all-start.2 = ((bf16[4,72,1024]{2,1,0:T(8,128)(2,1)}), bf16[4,72,1024]{2,1,0:T(8,128)(2,1)S(1)}, u32[]{:S(2)}, u32[]{:S(2)}) async-start(bf16[4,72,1024]{2,1,0:T(8,128)(2,1)} %convert_element_type.94), calls=%async_computation.3 | async-start | bytes 1179648 | tf_op jit(solution)/shard_map/all_to_all | solution.py:86
Sparse Core Ops, SparseCore 0:
  13.2 25.4 all-gather.2
  91.9 33.8 reduce-scatter.3
  128.1 76.7 reduce-scatter.5
where the time goes:
time: 215 us; the launch traced here: 214 us
  waiting for transfers between devices  145 us (67%)
  matrix products  15.3 us (7%)
  blocking collectives  15.3 us (7%)
  between operations  14.5 us (7%)
  starting transfers between devices  10.3 us (5%)
  other arithmetic  9.34 us (4%)
  local copies, waits for them, and re-layouts  4.69 us (2%)
    reduce_scatter x1, waiting for transfers between devices, on_device(): lax.psum_scatter(lax.dot_general(input_rows, delta_rows, (((0,), (0,)), (...  62.9 us
    reduce_scatter x1, waiting for transfers between devices, on_device(): lax.psum_scatter(grad_part.reshape(experts, halves * capacity, model_widt...  28.9 us
    all_gather x1, waiting for transfers between devices, on_device(): lax.all_gather(send_rows, 'seq', axis=1, tiled=True)  25.6 us
    all_to_all x1, waiting for transfers between devices, on_device(): lax.all_to_all(group_rows, 'expert', split_axis=0, concat_axis=0, tiled=T...  14.6 us
    all_to_all x1, waiting for transfers between devices, on_device(): lax.all_to_all(summed_rows.astype(jnp.bfloat16), 'expert', split_axis=0,...  8.96 us
    all_to_all x1, blocking collectives, on_device(): lax.all_to_all(group_gates, 'expert', split_axis=0, concat_axis=0, tiled=...  6.12 us
    dot_general x1, matrix products, on_device(): lax.dot_general(input_rows, delta_rows, (((0,), (0,)), ((), ())), preferr...  5.03 us
    unnamed x1, blocking collectives  4.92 us
  transfers between devices with their start and end apart: 6, of which 6 were waited for; matrix products, arithmetic and copies ran while one was open for 4% of the time, Pallas kernels for 0%

commit v1 on v0

v1 whole, which is shorter than its diff:
```python
import jax
import jax.numpy as jnp
from jax import lax
from jax.sharding import PartitionSpec as P

GATE_ROWS = 8


def slot_targets(block_routes, experts, capacity):
    flat_routes = block_routes.reshape(-1)
    one_hot = (flat_routes[:, None] == jnp.arange(experts, dtype=jnp.int32)[None, :]).astype(
        jnp.int32
    )
    before = jnp.cumsum(one_hot, axis=0) - one_hot
    slot_rank = jnp.sum(before * one_hot, axis=1)
    return (flat_routes * capacity + slot_rank).reshape(block_routes.shape)


def silu_parts(preact):
    sigma = jax.nn.sigmoid(preact)
    return (preact * sigma, sigma * (1.0 + preact * (1.0 - sigma)))


def gate_block(values, model_width):
    capacity = values.shape[-1]
    lead = values.ndim - 1
    padded = jnp.pad(
        values[..., None, :],
        [(0, 0)] * lead + [(0, GATE_ROWS - 1), (0, model_width - capacity)],
    )
    return padded


def seq_swap(x):
    return lax.ppermute(x, "seq", [(0, 1), (1, 0)])


def on_device(out_grad, routes, gates, saved_input, saved_preact, w_in, w_out):
    model_width = out_grad.shape[1]
    experts = lax.axis_size("expert")
    halves = lax.axis_size("seq")
    data_groups = lax.axis_size("dp")
    capacity = saved_input.shape[4]
    rows_per = capacity + GATE_ROWS
    cell_ids = jnp.arange(experts * capacity, dtype=jnp.int32)
    targets = slot_targets(routes, experts, capacity)
    first_pick = targets[:, 0][None, :] == cell_ids[:, None]
    second = targets[:, 1][None, :] == cell_ids[:, None]
    send_matrix = (first_pick | second).astype(jnp.bfloat16)
    send_rows = jnp.dot(send_matrix, out_grad, preferred_element_type=jnp.float32)
    send_rows = send_rows.astype(jnp.bfloat16).reshape(experts, capacity, model_width)
    gate_cells = jnp.sum(
        jnp.where(first_pick, gates[:, 0][None, :].astype(jnp.float32), 0.0)
        + jnp.where(second, gates[:, 1][None, :].astype(jnp.float32), 0.0),
        axis=1,
    )
    gate_cells = gate_cells.astype(jnp.bfloat16).reshape(experts, capacity)
    payload = jnp.concatenate([send_rows, gate_block(gate_cells, model_width)], axis=1)

    if halves == 2:
        seq_pos = lax.axis_index("seq")
        other = seq_swap(payload)
        group = jnp.where(
            seq_pos == 0, jnp.stack([payload, other], axis=1), jnp.stack([other, payload], axis=1)
        )
    else:
        group = lax.all_gather(payload, "seq", axis=1, tiled=False)
    group = lax.all_to_all(group, "expert", split_axis=0, concat_axis=0, tiled=True)
    row_count = experts * halves * capacity
    flat_rows = group[:, :, :capacity, :].reshape(row_count, model_width)
    flat_gates = group[:, :, capacity, :capacity].reshape(row_count, 1).astype(jnp.float32)
    input_rows = saved_input.reshape(row_count, model_width)
    preact_rows = saved_preact.reshape(row_count, -1).astype(jnp.float32)
    w_in_half = w_in[0]
    w_out_half = w_out[0]
    raw_grad = lax.dot_general(
        flat_rows, w_out_half, (((1,), (1,)), ((), ())), preferred_element_type=jnp.float32
    )
    activation, slope = silu_parts(preact_rows)
    gate_part = jnp.sum(activation * raw_grad, axis=1)
    delta_rows = (flat_gates * raw_grad * slope).astype(jnp.bfloat16)
    weight_part = lax.dot_general(
        input_rows, delta_rows, (((0,), (0,)), ((), ())), preferred_element_type=jnp.float32
    )
    weight_share = lax.psum_scatter(
        (weight_part * (1.0 / data_groups)).astype(jnp.bfloat16),
        "dp",
        scatter_dimension=0,
        tiled=True,
    )
    weight_grad = weight_share.astype(jnp.float32)[None]
    grad_part = lax.dot_general(
        delta_rows, w_in_half, (((1,), (1,)), ((), ())), preferred_element_type=jnp.float32
    )
    back = jnp.concatenate(
        [
            grad_part.reshape(experts, halves, capacity, model_width),
            gate_block(gate_part.reshape(experts, halves, capacity), model_width),
        ],
        axis=2,
    )
    if halves == 2:
        mine = jnp.where(seq_pos == 0, back[:, 0], back[:, 1])
        theirs = jnp.where(seq_pos == 0, back[:, 1], back[:, 0])
        received = seq_swap(theirs.astype(jnp.bfloat16))
        summed = (mine + received.astype(jnp.float32)).astype(jnp.bfloat16)
    else:
        summed = lax.psum_scatter(back, "seq", scatter_dimension=1, tiled=True)
        summed = summed.reshape(experts, rows_per, model_width).astype(jnp.bfloat16)
    back_rows = lax.all_to_all(summed, "expert", split_axis=0, concat_axis=0, tiled=True)
    back_flat = back_rows[:, :capacity, :].reshape(experts * capacity, model_width)
    input_grad = lax.dot_general(
        send_matrix, back_flat, (((0,), (0,)), ((), ())), preferred_element_type=jnp.float32
    ).astype(jnp.bfloat16)
    gate_values = back_rows[:, capacity, :capacity].reshape(experts * capacity).astype(jnp.float32)
    gate_first = jnp.sum(jnp.where(first_pick, gate_values[:, None], 0.0), axis=0)
    gate_second = jnp.sum(jnp.where(second, gate_values[:, None], 0.0), axis=0)
    gate_grad = jnp.stack([gate_first, gate_second], axis=1).astype(jnp.bfloat16)
    return (input_grad, gate_grad, weight_grad)


def solution(mesh):
    return jax.shard_map(
        on_device,
        mesh=mesh,
        in_specs=(
            P(("dp", "seq", "expert"), None),
            P(("dp", "seq", "expert"), None),
            P(("dp", "seq", "expert"), None),
            P("dp", "expert", None, None, None, None),
            P("dp", "expert", None, None, None, "seq"),
            P("expert", None, "seq"),
            P("expert", "seq", None),
        ),
        out_specs=(
            P(("dp", "seq", "expert"), None),
            P(("dp", "seq", "expert"), None),
            P("expert", "dp", "seq"),
        ),
        check_vma=False,
    )
```

time: 215 us -> 114 us (0.53)
  waiting for transfers between devices: 145 us -> 38.9 us
  blocking collectives: 15.3 us -> 32.6 us
  starting transfers between devices: 10.3 us -> 4.69 us
  matrix products: 15.3 us -> 11.2 us
    reduce_scatter x2 -> x1, waiting for transfers between devices: 91.8 us -> 9.43 us  [on_device(): lax.psum_scatter((weight_part * (1.0 / data_groups)).astype(jnp.bfloat16)...]
    ppermute x0 -> x2, waiting for transfers between devices: none -> 29.4 us  [seq_swap(): return lax.ppermute(x, 'seq', [(0, 1), (1, 0)])]
    all_to_all x3 -> x0, waiting for transfers between devices: 27.1 us -> none  [the longest x1 14.6 us: on_device(): lax.all_to_all(group_rows, 'expert', split_axis=0, concat_axis=0, tiled=T...]
    all_to_all x1 -> x2, blocking collectives: 6.12 us -> 32.6 us  [the longest x1 20 us: on_device(): lax.all_to_all(group, 'expert', split_axis=0, concat_axis=0, tiled=True)]
    all_gather x1 -> x0, waiting for transfers between devices: 25.6 us -> none  [on_device(): lax.all_gather(send_rows, 'seq', axis=1, tiled=True)]
    all_to_all x3 -> x0, starting transfers between devices: 10.2 us -> none  [the longest x1 3.53 us: on_device(): lax.all_to_all(group_rows, 'expert', split_axis=0, concat_axis=0, tiled=T...]
    unnamed x1 -> x0, blocking collectives: 4.92 us -> none
    convert_element_type x4, other arithmetic: 5.25 us -> 0.54 us  [the longest x1 0.38 us: on_device(): summed = (mine + received.astype(jnp.float32)).astype(jnp.bfloat16)]
  transfers between devices with their start and end apart: 6 -> 3, of which waited for: 6 -> 3; matrix products, arithmetic and copies ran while one was open for 4% -> 5% of each run, Pallas kernels for 0% -> 0%
where the time goes in v1:
time: 114 us
  waiting for transfers between devices  38.9 us (34%)
  blocking collectives  32.6 us (29%)
  between operations  14.2 us (12%)
  matrix products  11.2 us (10%)
  other arithmetic  7.27 us (6%)
  starting transfers between devices  4.69 us (4%)
  local copies, waits for them, and re-layouts  4.64 us (4%)
    ppermute x2, waiting for transfers between devices, seq_swap(): return lax.ppermute(x, 'seq', [(0, 1), (1, 0)])  29.4 us
    all_to_all x1, blocking collectives, on_device(): lax.all_to_all(group, 'expert', split_axis=0, concat_axis=0, tiled=True)  20 us
    all_to_all x1, blocking collectives, on_device(): lax.all_to_all(summed, 'expert', split_axis=0, concat_axis=0, tiled=True)  12.6 us
    reduce_scatter x1, waiting for transfers between devices, on_device(): lax.psum_scatter((weight_part * (1.0 / data_groups)).astype(jnp.bfloat16)...  9.43 us
    ppermute x2, starting transfers between devices, seq_swap(): return lax.ppermute(x, 'seq', [(0, 1), (1, 0)])  4.65 us
    unnamed x8, local copies, waits for them, and re-layouts  3.41 us
    dot_general x1, matrix products, on_device(): lax.dot_general(input_rows, delta_rows, (((0,), (0,)), ((), ())), preferr...  3.2 us
    dot_general x1, matrix products, on_device(): lax.dot_general(delta_rows, w_in_half, (((1,), (1,)), ((), ())), preferre...  3.02 us
  transfers between devices with their start and end apart: 3, of which 3 were waited for; matrix products, arithmetic and copies ran while one was open for 5% of the time, Pallas kernels for 0%

profile of v1, /device:TPU:0, one launch (start us, length us, event | category | flops | bytes accessed | tf_op | source)
XLA Modules:
  0.0 113.5 jit_solution(9927624691153430665)
XLA Ops:
  7.2 0.9 copy.53
  8.4 0.7 bitcast_convert_fusion.2
  9.2 1.2 %reduce-window.6 = s32[4,2,128]{2,1,0:T(2,128)S(1)} reduce-window(s32[4,2,128]{2,1,0:T(2,128)S(1)} %compare_convert_fusion, s32[]{:T(128)} %constant.16.clone.1), window={size=1x1x128 pad=0_0x0_0x127_0}, to_apply=%region_0.0 | reduce-window | flops 130048 | bytes 8196 | tf_op jit(solution)/shard_map/reduce-window
  11.0 0.7 multiply_add_fusion
  12.0 1.3 %convolution_convert_fusion = bf16[288,1024]{1,0:T(8,128)(2,1)S(1)} fusion(bf16[128,1024]{1,0:T(8,128)(2,1)} %param.7, s32[128]{0:T(128)S(1)} %get-tuple-element.25, s32[128]{0:T(128)S(1)} %get-tuple-element.24), kind=kOutput, calls=%fused_computation.20 | convolution fusion | flops 75902976 | bytes 852992 | tf_op jit(solution)/shard_map/dot_general | solution.py:50
  13.2 0.2 fusion.32
  13.4 3.1 %collective-permute-start = (bf16[4,80,1024]{2,1,0:T(8,128)(2,1)S(1)}, bf16[4,80,1024]{2,1,0:T(8,128)(2,1)}, u32[]{:S(2)}, u32[]{:S(2)}) collective-permute-start(bf16[4,80,1024]{2,1,0:T(8,128)(2,1)S(1)} %get-tuple-element.23), channel_id=1, source_target_pairs={{0,4},{4,0},{1,5},{5,1},{2,6},{6,2},{3,7},{7,3},{8,12},{12,8},{9,1... | collective-permute-start | bytes 1966088 | tf_op jit(solution)/shard_map/ppermute | solution.py:35
  16.5 14.8 %collective-permute-done = bf16[4,80,1024]{2,1,0:T(8,128)(2,1)} collective-permute-done((bf16[4,80,1024]{2,1,0:T(8,128)(2,1)S(1)}, bf16[4,80,1024]{2,1,0:T(8,128)(2,1)}, u32[]{:S(2)}, u32[]{:S(2)}) %collective-permute-start) | collective-permute-done | bytes 655392 | tf_op jit(solution)/shard_map/ppermute | solution.py:35
  31.3 1.5 %maximum_select_fusion = bf16[4,2,80,1024]{3,2,1,0:T(8,128)(2,1)S(1)} fusion(bf16[4,1,80,1024]{3,2,1,0:T(8,128)(2,1)} %bitcast.8, bf16[4,1,80,1024]{3,2,1,0:T(8,128)(2,1)S(1)} %get-tuple-element.22, pred[]{:T(512)S(6)} %eq.76), kind=kLoop, calls=%fused_computation.22 | loop fusion | flops 1966080 | bytes 2621441 | tf_op jit(solution)/shard_map/jit(_where)/select_n | solution.py:63
  32.8 20.0 %all_to_all.10 = bf16[4,2,80,1024]{3,2,1,0:T(8,128)(2,1)S(1)} all-to-all(bf16[4,2,80,1024]{3,2,1,0:T(8,128)(2,1)S(1)} %maximum_select_fusion), channel_id=1, replica_groups=mesh['dp'=4,'seq'=2,'expert'=4] {'expert'}, dimensions={0} | all-to-all | bytes 2621440 | tf_op jit(solution)/shard_map/all_to_all | solution.py:68
  53.0 1.2 %copy-done.1 = bf16[1,1,4,2,72,1024]{5,4,3,2,1,0:T(8,128)(2,1)S(1)} copy-done((bf16[1,1,4,2,72,1024]{5,4,3,2,1,0:T(8,128)(2,1)S(1)}, bf16[1,1,4,2,72,1024]{5,4,3,2,1,0:T(8,128)(2,1)}, u32[]{:S(2)}) %copy-start.1) | copy-done | bytes 1179672
  54.2 2.7 %fusion.6 = (bf16[576,1024]{1,0:T(8,128)(2,1)S(1)}, f32[576]{0:T(1024)S(1)}) fusion(f32[576]{0:T(1024)S(1)} %reshape.102, bf16[1,1,4,2,72,1024]{5,4,3,2,1,0:T(8,128)(2,1)S(1)} %copy-done.1, bf16[576,1024]{1,0:T(8,128)(2,1)S(1)} %bitcast.99, bf16[576,1024]{1,0:T(8,128)(2,1)S(1)} %bitcast.95, bf16[1,1024,1024]{2,1,0:T(8,128)(2,1)S(1)} %copy-done), kind=kOutput, calls=%fused_computation.12 | convolution fusion | flops 1218575872 | bytes 6820352 | tf_op jit(solution)/shard_map/dot_general | solution.py:76
  56.9 3.2 %fusion.13 = bf16[1024,1024]{0,1:T(8,128)(2,1)} fusion(bf16[576,1024]{1,0:T(8,128)(2,1)S(1)} %get-tuple-element.20, bf16[576,1024]{1,0:T(8,128)(2,1)S(1)} %bitcast.100), kind=kOutput, calls=%fused_computation.19 | convolution fusion | flops 1210056704 | bytes 4456448 | tf_op jit(solution)/shard_map/dot_general | solution.py:82
  60.2 3.0 %fusion.9 = f32[4,2,72,1024]{3,2,1,0:T(8,128)S(1)} fusion(bf16[4,2,72,1024]{3,2,1,0:T(8,128)(2,1)S(1)} %bitcast.101, bf16[1,1024,1024]{2,1,0:T(8,128)(2,1)} %param.12), kind=kOutput, calls=%fused_computation.15 | convolution fusion | flops 1207959552 | bytes 5636096 | tf_op jit(solution)/shard_map/dot_general | solution.py:92
  63.2 0.4 select_maximum_fusion
  63.8 1.6 %collective-permute-start.1 = (bf16[4,80,1024]{2,1,0:T(8,128)(2,1)S(1)}, bf16[4,80,1024]{2,1,0:T(8,128)(2,1)S(1)}, u32[]{:S(2)}, u32[]{:S(2)}) collective-permute-start(bf16[4,80,1024]{2,1,0:T(8,128)(2,1)S(1)} %fusion.19), channel_id=1, source_target_pairs={{0,4},{4,0},{1,5},{5,1},{2,6},{6,2},{3,7},{7,3},{8,12},{12,8},{9,1... | collective-permute-start | bytes 1966088 | tf_op jit(solution)/shard_map/ppermute | solution.py:35
  65.4 14.6 %collective-permute-done.1 = bf16[4,80,1024]{2,1,0:T(8,128)(2,1)S(1)} collective-permute-done((bf16[4,80,1024]{2,1,0:T(8,128)(2,1)S(1)}, bf16[4,80,1024]{2,1,0:T(8,128)(2,1)S(1)}, u32[]{:S(2)}, u32[]{:S(2)}) %collective-permute-start.1) | collective-permute-done | bytes 655392 | tf_op jit(solution)/shard_map/ppermute | solution.py:35
  79.9 0.4 fusion.16
  80.3 12.6 %all_to_all.11 = bf16[4,80,1024]{2,1,0:T(8,128)(2,1)S(1)} all-to-all(bf16[4,80,1024]{2,1,0:T(8,128)(2,1)S(1)} %fusion.16), channel_id=1, replica_groups=mesh['dp'=4,'seq'=2,'expert'=4] {'expert'}, dimensions={0} | all-to-all | bytes 1310720 | tf_op jit(solution)/shard_map/all_to_all | solution.py:110
  93.2 0.5 pad_maximum_fusion
  93.7 1.1 convolution_convert_fusion.1
  94.8 9.4 %reduce-scatter.2.cloned.1.call-done = bf16[256,1024]{0,1:T(8,128)(2,1)} async-done(((bf16[1024,1024]{0,1:T(8,128)(2,1)}), bf16[256,1024]{0,1:T(8,128)(2,1)}) %reduce-scatter.2.cloned.1.call-update) | async-done | bytes 524304 | tf_op jit(solution)/shard_map/reduce_scatter | solution.py:85
  104.2 1.1 bitcast_convert_fusion
  105.4 1.3 %copy.63 = f32[1,256,1024]{2,1,0:T(8,128)} copy(f32[1,256,1024]{1,2,0:T(8,128)S(1)} %bitcast_convert_fusion) | data formatting | bytes 2097152
  (31 shorter events, 1.9 us)
Async XLA Ops:
  7.2 45.8 %copy-start = (bf16[1,1024,1024]{2,1,0:T(8,128)(2,1)S(1)}, bf16[1,1024,1024]{2,1,0:T(8,128)(2,1)}, u32[]{:S(2)}) copy-start(bf16[1,1024,1024]{2,1,0:T(8,128)(2,1)} %param.13) | copy-start | bytes 6291460
  7.2 97.1 %reduce-scatter.2.cloned.1.call-start = ((), (), s32[]{:S(2)}) async-start(), calls=%async_computation.3 | async-start | bytes 2621440 | tf_op jit(solution)/shard_map/reduce_scatter | solution.py:85
  13.4 17.9 %collective-permute-start = (bf16[4,80,1024]{2,1,0:T(8,128)(2,1)S(1)}, bf16[4,80,1024]{2,1,0:T(8,128)(2,1)}, u32[]{:S(2)}, u32[]{:S(2)}) collective-permute-start(bf16[4,80,1024]{2,1,0:T(8,128)(2,1)S(1)} %get-tuple-element.23), channel_id=1, source_target_pairs={{0,4},{4,0},{1,5},{5,1},{2,6},{6,2},{3,7},{7,3},{8,12},{12,8},{9,1... | collective-permute-start | bytes 1966088 | tf_op jit(solution)/shard_map/ppermute | solution.py:35
  52.9 1.3 %copy-start.1 = (bf16[1,1,4,2,72,1024]{5,4,3,2,1,0:T(8,128)(2,1)S(1)}, bf16[1,1,4,2,72,1024]{5,4,3,2,1,0:T(8,128)(2,1)}, u32[]{:S(2)}) copy-start(bf16[1,1,4,2,72,1024]{5,4,3,2,1,0:T(8,128)(2,1)} %param.11) | copy-start | bytes 3538948
  54.2 2.7 %copy-start.2 = (bf16[1,1,4,2,72,1024]{5,4,3,2,1,0:T(8,128)(2,1)S(1)}, bf16[1,1,4,2,72,1024]{5,4,3,2,1,0:T(8,128)(2,1)}, u32[]{:S(2)}) copy-start(bf16[1,1,4,2,72,1024]{5,4,3,2,1,0:T(8,128)(2,1)} %param.10) | copy-start | bytes 3538948
  63.8 16.2 %collective-permute-start.1 = (bf16[4,80,1024]{2,1,0:T(8,128)(2,1)S(1)}, bf16[4,80,1024]{2,1,0:T(8,128)(2,1)S(1)}, u32[]{:S(2)}, u32[]{:S(2)}) collective-permute-start(bf16[4,80,1024]{2,1,0:T(8,128)(2,1)S(1)} %fusion.19), channel_id=1, source_target_pairs={{0,4},{4,0},{1,5},{5,1},{2,6},{6,2},{3,7},{7,3},{8,12},{12,8},{9,1... | collective-permute-start | bytes 1966088 | tf_op jit(solution)/shard_map/ppermute | solution.py:35
Sparse Core Ops, SparseCore 0:
  60.3 43.9 reduce-scatter.1

commit v2 on v1

--- a/solution.py
+++ b/solution.py
@@ -35,13 +35,42 @@
     return lax.ppermute(x, "seq", [(0, 1), (1, 0)])
 
 
+def expert_rows(block, input_rows, preact_rows, w_in_half, w_out_half):
+    sources, capacity, model_width = input_rows.shape
+    count = sources * capacity
+    rows = block[:, :capacity, :].reshape(count, model_width)
+    row_gates = block[:, capacity, :capacity].reshape(count, 1).astype(jnp.float32)
+    raw_grad = lax.dot_general(
+        rows, w_out_half, (((1,), (1,)), ((), ())), preferred_element_type=jnp.float32
+    )
+    activation, slope = silu_parts(preact_rows.reshape(count, -1).astype(jnp.float32))
+    gate_part = jnp.sum(activation * raw_grad, axis=1)
+    delta_rows = (row_gates * raw_grad * slope).astype(jnp.bfloat16)
+    grad_part = lax.dot_general(
+        delta_rows, w_in_half, (((1,), (1,)), ((), ())), preferred_element_type=jnp.float32
+    )
+    back = jnp.concatenate(
+        [
+            grad_part.reshape(sources, capacity, model_width),
+            gate_block(gate_part.reshape(sources, capacity), model_width),
+        ],
+        axis=1,
+    )
+    weight_part = lax.dot_general(
+        input_rows.reshape(count, model_width),
+        delta_rows,
+        (((0,), (0,)), ((), ())),
+        preferred_element_type=jnp.float32,
+    )
+    return back, weight_part
+
+
 def on_device(out_grad, routes, gates, saved_input, saved_preact, w_in, w_out):
     model_width = out_grad.shape[1]
     experts = lax.axis_size("expert")
     halves = lax.axis_size("seq")
     data_groups = lax.axis_size("dp")
     capacity = saved_input.shape[4]
-    rows_per = capacity + GATE_ROWS
     cell_ids = jnp.arange(experts * capacity, dtype=jnp.int32)
     targets = slot_targets(routes, experts, capacity)
     first_pick = targets[:, 0][None, :] == cell_ids[:, None]
@@ -56,32 +85,45 @@
     )
     gate_cells = gate_cells.astype(jnp.bfloat16).reshape(experts, capacity)
     payload = jnp.concatenate([send_rows, gate_block(gate_cells, model_width)], axis=1)
-
+    same = lax.all_to_all(payload, "expert", split_axis=0, concat_axis=0, tiled=True)
+    w_in_half = w_in[0]
+    w_out_half = w_out[0]
+    inputs = saved_input[0, 0]
+    preacts = saved_preact[0, 0]
     if halves == 2:
         seq_pos = lax.axis_index("seq")
-        other = seq_swap(payload)
-        group = jnp.where(
-            seq_pos == 0, jnp.stack([payload, other], axis=1), jnp.stack([other, payload], axis=1)
+        other = seq_swap(same)
+        own_back, own_weight = expert_rows(
+            same,
+            lax.dynamic_index_in_dim(inputs, seq_pos, axis=1, keepdims=False),
+            lax.dynamic_index_in_dim(preacts, seq_pos, axis=1, keepdims=False),
+            w_in_half,
+            w_out_half,
         )
+        far_back, far_weight = expert_rows(
+            other,
+            lax.dynamic_index_in_dim(inputs, 1 - seq_pos, axis=1, keepdims=False),
+            lax.dynamic_index_in_dim(preacts, 1 - seq_pos, axis=1, keepdims=False),
+            w_in_half,
+            w_out_half,
+        )
+        received = seq_swap(far_back.astype(jnp.bfloat16))
+        summed = (own_back + received.astype(jnp.float32)).astype(jnp.bfloat16)
+        weight_part = own_weight + far_weight
     else:
-        group = lax.all_gather(payload, "seq", axis=1, tiled=False)
-    group = lax.all_to_all(group, "expert", split_axis=0, concat_axis=0, tiled=True)
-    row_count = experts * halves * capacity
-    flat_rows = group[:, :, :capacity, :].reshape(row_count, model_width)
-    flat_gates = group[:, :, capacity, :capacity].reshape(row_count, 1).astype(jnp.float32)
-    input_rows = saved_input.reshape(row_count, model_width)
-    preact_rows = saved_preact.reshape(row_count, -1).astype(jnp.float32)
-    w_in_half = w_in[0]
-    w_out_half = w_out[0]
-    raw_grad = lax.dot_general(
-        flat_rows, w_out_half, (((1,), (1,)), ((), ())), preferred_element_type=jnp.float32
-    )
-    activation, slope = silu_parts(preact_rows)
-    gate_part = jnp.sum(activation * raw_grad, axis=1)
-    delta_rows = (flat_gates * raw_grad * slope).astype(jnp.bfloat16)
-    weight_part = lax.dot_general(
-        input_rows, delta_rows, (((0,), (0,)), ((), ())), preferred_element_type=jnp.float32
-    )
+        group = lax.all_gather(same, "seq", axis=1, tiled=False)
+        sources = group.shape[0]
+        flat = group.reshape(sources * halves, -1, model_width)
+        back, weight_part = expert_rows(
+            flat,
+            inputs.reshape(sources * halves, capacity, model_width),
+            preacts.reshape(sources * halves, capacity, -1),
+            w_in_half,
+            w_out_half,
+        )
+        back = back.reshape(sources, halves, -1, model_width)
+        summed = lax.psum_scatter(back, "seq", scatter_dimension=1, tiled=True)
+        summed = summed.reshape(sources, -1, model_width).astype(jnp.bfloat16)
     weight_share = lax.psum_scatter(
         (weight_part * (1.0 / data_groups)).astype(jnp.bfloat16),
         "dp",
@@ -89,24 +131,6 @@
         tiled=True,
     )
     weight_grad = weight_share.astype(jnp.float32)[None]
-    grad_part = lax.dot_general(
-        delta_rows, w_in_half, (((1,), (1,)), ((), ())), preferred_element_type=jnp.float32
-    )
-    back = jnp.concatenate(
-        [
-            grad_part.reshape(experts, halves, capacity, model_width),
-            gate_block(gate_part.reshape(experts, halves, capacity), model_width),
-        ],
-        axis=2,
-    )
-    if halves == 2:
-        mine = jnp.where(seq_pos == 0, back[:, 0], back[:, 1])
-        theirs = jnp.where(seq_pos == 0, back[:, 1], back[:, 0])
-        received = seq_swap(theirs.astype(jnp.bfloat16))
-        summed = (mine + received.astype(jnp.float32)).astype(jnp.bfloat16)
-    else:
-        summed = lax.psum_scatter(back, "seq", scatter_dimension=1, tiled=True)
-        summed = summed.reshape(experts, rows_per, model_width).astype(jnp.bfloat16)
     back_rows = lax.all_to_all(summed, "expert", split_axis=0, concat_axis=0, tiled=True)
     back_flat = back_rows[:, :capacity, :].reshape(experts * capacity, model_width)
     input_grad = lax.dot_general(

time: 114 us -> 107 us (0.939)
  blocking collectives: 32.6 us -> 12.6 us
  matrix products: 11.2 us -> 17.7 us
  starting transfers between devices: 4.69 us -> 8.33 us
  local copies, waits for them, and re-layouts: 4.64 us -> 7.55 us
    all_to_all x1 -> x0, blocking collectives: 20 us -> none  [on_device(): lax.all_to_all(group, 'expert', split_axis=0, concat_axis=0, tiled=True)]
    ppermute x2, waiting for transfers between devices: 29.4 us -> 20.8 us  [seq_swap(): return lax.ppermute(x, 'seq', [(0, 1), (1, 0)])]
    all_to_all x0 -> x1, waiting for transfers between devices: none -> 6.79 us  [on_device(): lax.all_to_all(payload, 'expert', split_axis=0, concat_axis=0, tiled=True)]
    dot_general x3 -> x6, matrix products: 8.93 us -> 15.4 us  [the longest x2 5.95 us: expert_rows(): lax.dot_general(input_rows.reshape(count, model_width), delta_rows, (((0,...]
    all_to_all x0 -> x1, starting transfers between devices: none -> 4.23 us  [on_device(): lax.all_to_all(payload, 'expert', split_axis=0, concat_axis=0, tiled=True)]
    dynamic_slice x0 -> x2, local copies, waits for them, and re-layouts: none -> 3.42 us  [the longest x1 2.27 us: on_device(): lax.dynamic_index_in_dim(inputs, 1 - seq_pos, axis=1, keepdims=False)]
    reduce_scatter x1, waiting for transfers between devices: 9.43 us -> 11.6 us  [on_device(): lax.psum_scatter((weight_part * (1.0 / data_groups)).astype(jnp.bfloat16)...]
    unnamed x8 -> x15, local copies, waits for them, and re-layouts: 3.41 us -> 1.8 us
  transfers between devices with their start and end apart: 3 -> 4, of which waited for: 3 -> 4; matrix products, arithmetic and copies ran while one was open for 5% -> 15% of each run, Pallas kernels for 0% -> 0%
where the time goes in v2:
time: 107 us
  waiting for transfers between devices  39.2 us (37%)
  matrix products  17.7 us (17%)
  between operations  14.1 us (13%)
  blocking collectives  12.6 us (12%)
  starting transfers between devices  8.33 us (8%)
  local copies, waits for them, and re-layouts  7.55 us (7%)
  other arithmetic  6.93 us (6%)
    ppermute x2, waiting for transfers between devices, seq_swap(): return lax.ppermute(x, 'seq', [(0, 1), (1, 0)])  20.8 us
    all_to_all x1, blocking collectives, on_device(): lax.all_to_all(summed, 'expert', split_axis=0, concat_axis=0, tiled=True)  12.6 us
    reduce_scatter x1, waiting for transfers between devices, on_device(): lax.psum_scatter((weight_part * (1.0 / data_groups)).astype(jnp.bfloat16)...  11.6 us
    all_to_all x1, waiting for transfers between devices, on_device(): lax.all_to_all(payload, 'expert', split_axis=0, concat_axis=0, tiled=True)  6.79 us
    dot_general x2, matrix products, expert_rows(): lax.dot_general(input_rows.reshape(count, model_width), delta_rows, (((0,...  5.95 us
    dot_general x2, matrix products, expert_rows(): lax.dot_general(delta_rows, w_in_half, (((1,), (1,)), ((), ())), preferre...  5.01 us
    dot_general x2, matrix products, expert_rows(): lax.dot_general(rows, w_out_half, (((1,), (1,)), ((), ())), preferred_ele...  4.47 us
    all_to_all x1, starting transfers between devices, on_device(): lax.all_to_all(payload, 'expert', split_axis=0, concat_axis=0, tiled=True)  4.23 us
  transfers between devices with their start and end apart: 4, of which 4 were waited for; matrix products, arithmetic and copies ran while one was open for 15% of the time, Pallas kernels for 0%

profile of v2, /device:TPU:0, one launch (start us, length us, event | category | flops | bytes accessed | tf_op | source)
XLA Modules:
  0.0 106.5 jit_solution(9850117185883428136)
XLA Ops:
  7.2 0.9 copy.36
  9.1 1.2 %reduce-window.6 = s32[4,2,128]{2,1,0:T(2,128)S(1)} reduce-window(s32[4,2,128]{2,1,0:T(2,128)S(1)} %compare_convert_fusion, s32[]{:T(128)} %constant.33.clone.1), window={size=1x1x128 pad=0_0x0_0x127_0}, to_apply=%region_0.0 | reduce-window | flops 130048 | bytes 8196 | tf_op jit(solution)/shard_map/reduce-window
  11.9 1.3 %convolution_convert_fusion = bf16[288,1024]{1,0:T(8,128)(2,1)S(1)} fusion(bf16[128,1024]{1,0:T(8,128)(2,1)} %param.7, s32[128]{0:T(128)S(1)} %get-tuple-element.14, s32[128]{0:T(128)S(1)} %get-tuple-element.13), kind=kOutput, calls=%fused_computation.15 | convolution fusion | flops 75902976 | bytes 852992 | tf_op jit(solution)/shard_map/dot_general | solution.py:79
  13.2 0.9 fusion.33
  14.1 4.2 %all-to-all-start = ((bf16[4,80,1024]{2,1,0:T(8,128)(2,1)}), bf16[4,80,1024]{2,1,0:T(8,128)(2,1)S(1)}, u32[]{:S(2)}, u32[]{:S(2)}) async-start(bf16[4,80,1024]{2,1,0:T(8,128)(2,1)} %fusion.33), calls=%async_computation | async-start | bytes 1310720 | tf_op jit(solution)/shard_map/all_to_all | solution.py:88
  18.3 2.3 %constant_dynamic-slice_fusion.3 = (bf16[1,1,4,1,72,1024]{5,4,3,2,1,0:T(8,128)(2,1)}, bf16[1,1,4,1,72,1024]{5,4,3,2,1,0:T(8,128)(2,1)S(1)}) fusion(bf16[1,1,4,2,72,1024]{5,4,3,2,1,0:T(8,128)(2,1)} %param.10, s32[]{:T(128)S(6)} %select_n.26, s32[]{:T(128)S(6)} %select_n.25), kind=kLoop, calls=%fused_computation.71 | loop fusion | bytes 2359304 | tf_op jit(solution)/shard_map/jit(dynamic_index_in_dim)/dynamic_slice | solution.py:105
  20.6 1.2 %constant_dynamic-slice_fusion.1 = (bf16[1,1,4,1,72,1024]{5,4,3,2,1,0:T(8,128)(2,1)}, bf16[1,1,4,1,72,1024]{5,4,3,2,1,0:T(8,128)(2,1)}) fusion(bf16[1,1,4,2,72,1024]{5,4,3,2,1,0:T(8,128)(2,1)S(1)} %copy-done.3, s32[]{:T(128)S(6)} %select_n.26, s32[]{:T(128)S(6)} %select_n.25), kind=kLoop, calls=%fused_computation.69 | loop fusion | bytes 2359304 | tf_op jit(solution)/shard_map/jit(dynamic_index_in_dim)/dynamic_slice | solution.py:106
  21.8 6.8 %all-to-all-done = bf16[4,80,1024]{2,1,0:T(8,128)(2,1)S(1)} async-done(((bf16[4,80,1024]{2,1,0:T(8,128)(2,1)}), bf16[4,80,1024]{2,1,0:T(8,128)(2,1)S(1)}, u32[]{:S(2)}, u32[]{:S(2)}) %all-to-all-start) | async-done | bytes 655392 | tf_op jit(solution)/shard_map/all_to_all | solution.py:88
  28.7 2.3 %collective-permute-start = (bf16[4,80,1024]{2,1,0:T(8,128)(2,1)S(1)}, bf16[4,80,1024]{2,1,0:T(8,128)(2,1)S(1)}, u32[]{:S(2)}, u32[]{:S(2)}) collective-permute-start(bf16[4,80,1024]{2,1,0:T(8,128)(2,1)S(1)} %all-to-all-done), channel_id=1, source_target_pairs={{0,4},{4,0},{1,5},{5,1},{2,6},{6,2},{3,7},{7,3},{8,12},{12,8},{9,1... | collective-permute-start | bytes 1966088 | tf_op jit(solution)/shard_map/ppermute | solution.py:35
  31.0 1.6 %fusion.21 = (bf16[288,1024]{1,0:T(8,128)(2,1)S(1)}, f32[288]{0:T(512)S(1)}) fusion(f32[288]{0:T(512)S(1)} %reshape.131, bf16[1,1,4,1,72,1024]{5,4,3,2,1,0:T(8,128)(2,1)S(1)} %copy-done.6, bf16[288,1024]{1,0:T(8,128)(2,1)S(1)} %bitcast.88, bf16[288,1024]{1,0:T(8,128)(2,1)S(1)} %bitcast.85, bf16[1,1024,1024]{2,1,0:T(8,128)(2,1)S(1)} %copy-done), kind=kOutput, calls=%fused_computation.30 | convolution fusion | flops 609287936 | bytes 4458752 | tf_op jit(solution)/shard_map/dot_general | solution.py:43
  32.6 3.2 %fusion.48 = f32[1024,1024]{1,0:T(8,128)} fusion(bf16[288,1024]{1,0:T(8,128)(2,1)S(1)} %bitcast.79, bf16[288,1024]{1,0:T(8,128)(2,1)S(1)} %get-tuple-element.11), kind=kOutput, calls=%fused_computation.80 | convolution fusion | flops 603979776 | bytes 5373952 | tf_op jit(solution)/shard_map/dot_general | solution.py:59
  35.8 9.6 %collective-permute-done = bf16[4,80,1024]{2,1,0:T(8,128)(2,1)S(1)} collective-permute-done((bf16[4,80,1024]{2,1,0:T(8,128)(2,1)S(1)}, bf16[4,80,1024]{2,1,0:T(8,128)(2,1)S(1)}, u32[]{:S(2)}, u32[]{:S(2)}) %collective-permute-start) | collective-permute-done | bytes 655392 | tf_op jit(solution)/shard_map/ppermute | solution.py:35
  45.4 0.8 copy-done.5
  46.4 1.0 slice-done
  47.4 2.9 %fusion.30 = (bf16[288,1024]{1,0:T(8,128)(2,1)S(1)}, bf16[288]{0:T(512)(128)(2,1)S(1)}) fusion(f32[288]{0:T(512)S(1)} %reshape.133, bf16[1,1,4,1,72,1024]{5,4,3,2,1,0:T(8,128)(2,1)} %get-tuple-element.9, bf16[288,1024]{1,0:T(8,128)(2,1)} %bitcast.87, bf16[288,1024]{1,0:T(8,128)(2,1)S(1)} %bitcast.86, bf16[1,1024,1024]{2,1,0:T(8,128)(2,1)S(1)} %copy-done), kind=kOutput, calls=%fused_computation.39 | convolution fusion | flops 609287936 | bytes 4458176 | tf_op jit(solution)/shard_map/dot_general | solution.py:43
  50.3 2.7 %multiply_convert_fusion = bf16[1024,1024]{1,0:T(8,128)(2,1)} fusion(f32[1024,1024]{1,0:T(8,128)S(1)} %copy-done.1, bf16[288,1024]{1,0:T(8,128)(2,1)S(1)} %bitcast.80, bf16[288,1024]{1,0:T(8,128)(2,1)S(1)} %get-tuple-element.7), kind=kOutput, calls=%fused_computation | convolution fusion | flops 607125504 | bytes 7471104 | tf_op jit(solution)/shard_map/dot_general | solution.py:59
  53.1 2.4 %fusion.8 = bf16[4,72,1024]{2,1,0:T(8,128)(2,1)S(1)} fusion(bf16[4,72,1024]{2,1,0:T(8,128)(2,1)S(1)} %bitcast.84, bf16[1,1024,1024]{2,1,0:T(8,128)(2,1)} %param.12), kind=kOutput, calls=%fused_computation.16 | convolution fusion | flops 604274688 | bytes 3276800 | tf_op jit(solution)/shard_map/dot_general | solution.py:49
  55.6 1.8 %collective-permute-start.1 = (bf16[4,80,1024]{2,1,0:T(8,128)(2,1)S(1)}, bf16[4,80,1024]{2,1,0:T(8,128)(2,1)S(1)}, u32[]{:S(2)}, u32[]{:S(2)}) collective-permute-start(bf16[4,80,1024]{2,1,0:T(8,128)(2,1)S(1)} %fusion.34), channel_id=1, source_target_pairs={{0,4},{4,0},{1,5},{5,1},{2,6},{6,2},{3,7},{7,3},{8,12},{12,8},{9,1... | collective-permute-start | bytes 1966088 | tf_op jit(solution)/shard_map/ppermute | solution.py:35
  57.5 2.6 %fusion.2 = f32[4,72,1024]{2,1,0:T(8,128)S(1)} fusion(bf16[4,72,1024]{2,1,0:T(8,128)(2,1)} %bitcast.83, bf16[1,1024,1024]{2,1,0:T(8,128)(2,1)} %param.12), kind=kOutput, calls=%fused_computation.3 | convolution fusion | flops 603979776 | bytes 3866624 | tf_op jit(solution)/shard_map/dot_general | solution.py:49
  60.1 11.2 %collective-permute-done.1 = bf16[4,80,1024]{2,1,0:T(8,128)(2,1)S(1)} collective-permute-done((bf16[4,80,1024]{2,1,0:T(8,128)(2,1)S(1)}, bf16[4,80,1024]{2,1,0:T(8,128)(2,1)S(1)}, u32[]{:S(2)}, u32[]{:S(2)}) %collective-permute-start.1) | collective-permute-done | bytes 655392 | tf_op jit(solution)/shard_map/ppermute | solution.py:35
  71.5 12.6 %all_to_all.10 = bf16[4,80,1024]{2,1,0:T(8,128)(2,1)S(1)} all-to-all(bf16[4,80,1024]{2,1,0:T(8,128)(2,1)S(1)} %fusion.12), channel_id=1, replica_groups=mesh['dp'=4,'seq'=2,'expert'=4] {'expert'}, dimensions={0} | all-to-all | bytes 1310720 | tf_op jit(solution)/shard_map/all_to_all | solution.py:134
  84.9 1.1 convolution_convert_fusion.1
  86.0 11.6 %reduce-scatter.2.cloned.1.call-done = bf16[256,1024]{1,0:T(8,128)(2,1)} async-done(((bf16[1024,1024]{1,0:T(8,128)(2,1)}), bf16[256,1024]{1,0:T(8,128)(2,1)}) %reduce-scatter.2.cloned.1.call-update) | async-done | bytes 524304 | tf_op jit(solution)/shard_map/reduce_scatter | solution.py:127
  97.5 2.1 %bitcast_convert_fusion = f32[1,256,1024]{2,1,0:T(8,128)} fusion(bf16[256,1024]{1,0:T(8,128)(2,1)} %reduce-scatter.2.cloned.1.call-done), kind=kLoop, calls=%fused_computation.44 | loop fusion | flops 262144 | bytes 1572864 | tf_op jit(solution)/shard_map/broadcast_in_dim | solution.py:133
  (47 shorter events, 4.1 us)
Async XLA Ops:
  7.2 23.8 %copy-start = (bf16[1,1024,1024]{2,1,0:T(8,128)(2,1)S(1)}, bf16[1,1024,1024]{2,1,0:T(8,128)(2,1)}, u32[]{:S(2)}) copy-start(bf16[1,1024,1024]{2,1,0:T(8,128)(2,1)} %param.13) | copy-start | bytes 6291460
  14.1 14.5 %all-to-all-start = ((bf16[4,80,1024]{2,1,0:T(8,128)(2,1)}), bf16[4,80,1024]{2,1,0:T(8,128)(2,1)S(1)}, u32[]{:S(2)}, u32[]{:S(2)}) async-start(bf16[4,80,1024]{2,1,0:T(8,128)(2,1)} %fusion.33), calls=%async_computation | async-start | bytes 1310720 | tf_op jit(solution)/shard_map/all_to_all | solution.py:88
  18.3 79.2 %reduce-scatter.2.cloned.1.call-start = ((), (), s32[]{:S(2)}) async-start(), calls=%async_computation.3 | async-start | bytes 2621440 | tf_op jit(solution)/shard_map/reduce_scatter | solution.py:127
  18.3 2.3 %copy-start.3 = (bf16[1,1,4,2,72,1024]{5,4,3,2,1,0:T(8,128)(2,1)S(1)}, bf16[1,1,4,2,72,1024]{5,4,3,2,1,0:T(8,128)(2,1)}, u32[]{:S(2)}) copy-start(bf16[1,1,4,2,72,1024]{5,4,3,2,1,0:T(8,128)(2,1)} %param.11) | copy-start | bytes 3538948
  28.7 2.3 %copy-start.6 = (bf16[1,1,4,1,72,1024]{5,4,3,2,1,0:T(8,128)(2,1)S(1)}, bf16[1,1,4,1,72,1024]{5,4,3,2,1,0:T(8,128)(2,1)}, u32[]{:S(2)}) copy-start(bf16[1,1,4,1,72,1024]{5,4,3,2,1,0:T(8,128)(2,1)} %get-tuple-element.10) | copy-start | bytes 1769476
  28.7 16.7 %collective-permute-start = (bf16[4,80,1024]{2,1,0:T(8,128)(2,1)S(1)}, bf16[4,80,1024]{2,1,0:T(8,128)(2,1)S(1)}, u32[]{:S(2)}, u32[]{:S(2)}) collective-permute-start(bf16[4,80,1024]{2,1,0:T(8,128)(2,1)S(1)} %all-to-all-done), channel_id=1, source_target_pairs={{0,4},{4,0},{1,5},{5,1},{2,6},{6,2},{3,7},{7,3},{8,12},{12,8},{9,1... | collective-permute-start | bytes 1966088 | tf_op jit(solution)/shard_map/ppermute | solution.py:35
  32.6 3.2 %copy-start.4 = (bf16[288,1024]{1,0:T(8,128)(2,1)}, bf16[288,1024]{1,0:T(8,128)(2,1)S(1)}, u32[]{:S(2)}) copy-start(bf16[288,1024]{1,0:T(8,128)(2,1)S(1)} %get-tuple-element.11) | copy-start | bytes 1769476
  45.4 0.8 copy-start.5
  46.3 1.1 slice-start
  47.3 2.9 %copy-start.1 = (f32[1024,1024]{1,0:T(8,128)S(1)}, f32[1024,1024]{1,0:T(8,128)}, u32[]{:S(2)}) copy-start(f32[1024,1024]{1,0:T(8,128)} %fusion.48) | copy-start | bytes 12582916
  47.3 2.9 %copy-start.2 = (bf16[1,1,4,1,72,1024]{5,4,3,2,1,0:T(8,128)(2,1)S(1)}, bf16[1,1,4,1,72,1024]{5,4,3,2,1,0:T(8,128)(2,1)}, u32[]{:S(2)}) copy-start(bf16[1,1,4,1,72,1024]{5,4,3,2,1,0:T(8,128)(2,1)} %get-tuple-element.5) | copy-start | bytes 1769476
  55.6 15.7 %collective-permute-start.1 = (bf16[4,80,1024]{2,1,0:T(8,128)(2,1)S(1)}, bf16[4,80,1024]{2,1,0:T(8,128)(2,1)S(1)}, u32[]{:S(2)}, u32[]{:S(2)}) collective-permute-start(bf16[4,80,1024]{2,1,0:T(8,128)(2,1)S(1)} %fusion.34), channel_id=1, source_target_pairs={{0,4},{4,0},{1,5},{5,1},{2,6},{6,2},{3,7},{7,3},{8,12},{12,8},{9,1... | collective-permute-start | bytes 1966088 | tf_op jit(solution)/shard_map/ppermute | solution.py:35
Sparse Core Ops, SparseCore 0:
  53.2 44.3 reduce-scatter.1

commit v3 on v2

--- a/solution.py
+++ b/solution.py
@@ -71,8 +71,11 @@
     halves = lax.axis_size("seq")
     data_groups = lax.axis_size("dp")
     capacity = saved_input.shape[4]
+    expert_pos = lax.axis_index("expert")
+    seq_pos = lax.axis_index("seq")
+    rel_routes = jnp.bitwise_xor(routes, expert_pos)
     cell_ids = jnp.arange(experts * capacity, dtype=jnp.int32)
-    targets = slot_targets(routes, experts, capacity)
+    targets = slot_targets(rel_routes, experts, capacity)
     first_pick = targets[:, 0][None, :] == cell_ids[:, None]
     second = targets[:, 1][None, :] == cell_ids[:, None]
     send_matrix = (first_pick | second).astype(jnp.bfloat16)
@@ -85,53 +88,55 @@
     )
     gate_cells = gate_cells.astype(jnp.bfloat16).reshape(experts, capacity)
     payload = jnp.concatenate([send_rows, gate_block(gate_cells, model_width)], axis=1)
-    same = lax.all_to_all(payload, "expert", split_axis=0, concat_axis=0, tiled=True)
+
+    def pairs(ds, k):
+        return [
+            (ss * experts + jj, (ss ^ ds) * experts + (jj ^ k))
+            for ss in range(halves)
+            for jj in range(experts)
+        ]
+
+    received = {}
+    for ds in range(halves):
+        for k in range(experts):
+            if ds == 0 and k == 0:
+                received[(ds, k)] = payload[0]
+            else:
+                received[(ds, k)] = lax.ppermute(payload[k], ("seq", "expert"), pairs(ds, k))
+    near = jnp.stack([received[(0, k)] for k in range(experts)])
+    far = jnp.stack([received[(1, k)] for k in range(experts)])
+    order = jnp.bitwise_xor(expert_pos, jnp.arange(experts, dtype=jnp.int32))
+    inputs = saved_input[0, 0]
+    preacts = saved_preact[0, 0]
+
+    def saved_rows(values, seq_index):
+        half = lax.dynamic_index_in_dim(values, seq_index, axis=1, keepdims=False)
+        return jnp.take(half, order, axis=0)
+
     w_in_half = w_in[0]
     w_out_half = w_out[0]
-    inputs = saved_input[0, 0]
-    preacts = saved_preact[0, 0]
-    if halves == 2:
-        seq_pos = lax.axis_index("seq")
-        other = seq_swap(same)
-        own_back, own_weight = expert_rows(
-            same,
-            lax.dynamic_index_in_dim(inputs, seq_pos, axis=1, keepdims=False),
-            lax.dynamic_index_in_dim(preacts, seq_pos, axis=1, keepdims=False),
-            w_in_half,
-            w_out_half,
-        )
-        far_back, far_weight = expert_rows(
-            other,
-            lax.dynamic_index_in_dim(inputs, 1 - seq_pos, axis=1, keepdims=False),
-            lax.dynamic_index_in_dim(preacts, 1 - seq_pos, axis=1, keepdims=False),
-            w_in_half,
-            w_out_half,
-        )
-        received = seq_swap(far_back.astype(jnp.bfloat16))
-        summed = (own_back + received.astype(jnp.float32)).astype(jnp.bfloat16)
-        weight_part = own_weight + far_weight
-    else:
-        group = lax.all_gather(same, "seq", axis=1, tiled=False)
-        sources = group.shape[0]
-        flat = group.reshape(sources * halves, -1, model_width)
-        back, weight_part = expert_rows(
-            flat,
-            inputs.reshape(sources * halves, capacity, model_width),
-            preacts.reshape(sources * halves, capacity, -1),
-            w_in_half,
-            w_out_half,
-        )
-        back = back.reshape(sources, halves, -1, model_width)
-        summed = lax.psum_scatter(back, "seq", scatter_dimension=1, tiled=True)
-        summed = summed.reshape(sources, -1, model_width).astype(jnp.bfloat16)
+    near_back, near_weight = expert_rows(
+        near, saved_rows(inputs, seq_pos), saved_rows(preacts, seq_pos), w_in_half, w_out_half
+    )
+    far_back, far_weight = expert_rows(
+        far, saved_rows(inputs, 1 - seq_pos), saved_rows(preacts, 1 - seq_pos), w_in_half, w_out_half
+    )
     weight_share = lax.psum_scatter(
-        (weight_part * (1.0 / data_groups)).astype(jnp.bfloat16),
+        ((near_weight + far_weight) * (1.0 / data_groups)).astype(jnp.bfloat16),
         "dp",
         scatter_dimension=0,
         tiled=True,
     )
     weight_grad = weight_share.astype(jnp.float32)[None]
-    back_rows = lax.all_to_all(summed, "expert", split_axis=0, concat_axis=0, tiled=True)
+    back = [None] * experts
+    for k in range(experts):
+        partner_part = seq_swap(far_back[k].astype(jnp.bfloat16))
+        summed = (near_back[k] + partner_part.astype(jnp.float32)).astype(jnp.bfloat16)
+        if k == 0:
+            back[k] = summed
+        else:
+            back[k] = lax.ppermute(summed, "expert", [(jj, jj ^ k) for jj in range(experts)])
+    back_rows = jnp.stack(back)
     back_flat = back_rows[:, :capacity, :].reshape(experts * capacity, model_width)
     input_grad = lax.dot_general(
         send_matrix, back_flat, (((0,), (0,)), ((), ())), preferred_element_type=jnp.float32

time: 107 us -> 106 us (level)
  blocking collectives: 12.6 us -> 0 us
  other arithmetic: 6.93 us -> 14.7 us
  local copies, waits for them, and re-layouts: 7.55 us -> 14.8 us
  starting transfers between devices: 8.33 us -> 13.9 us
  waiting for transfers between devices: 39.2 us -> 33.8 us
  matrix products: 17.7 us -> 14.2 us
    all_to_all x1 -> x0, blocking collectives: 12.6 us -> none  [on_device(): lax.all_to_all(summed, 'expert', split_axis=0, concat_axis=0, tiled=True)]
    ppermute x0 -> x10, waiting for transfers between devices: none -> 11 us  [the longest x3 8.12 us: on_device(): lax.ppermute(summed, 'expert', [(jj, jj ^ k) for jj in range(experts)])]
    ppermute x0 -> x10, starting transfers between devices: none -> 9.82 us  [the longest x7 7.86 us: on_device(): received[ds, k] = lax.ppermute(payload[k], ('seq', 'expert'), pairs(ds, k))]
    ppermute x2 -> x4, waiting for transfers between devices: 20.8 us -> 11.1 us  [seq_swap(): return lax.ppermute(x, 'seq', [(0, 1), (1, 0)])]
    gather x0 -> x4, local copies, waits for them, and re-layouts: none -> 7.74 us  [saved_rows(): return jnp.take(half, order, axis=0)]
    all_to_all x1 -> x0, waiting for transfers between devices: 6.79 us -> none  [on_device(): lax.all_to_all(payload, 'expert', split_axis=0, concat_axis=0, tiled=True)]
    another operation x2 -> x7, other arithmetic: 1.25 us -> 6.42 us  [the longest x1 1.9 us: on_device(): far = jnp.stack([received[1, k] for k in range(experts)])]
    all_to_all x1 -> x0, starting transfers between devices: 4.23 us -> none  [on_device(): lax.all_to_all(payload, 'expert', split_axis=0, concat_axis=0, tiled=True)]
  transfers between devices with their start and end apart: 4 -> 15, of which waited for: 4 -> 8; matrix products, arithmetic and copies ran while one was open for 15% -> 23% of each run, Pallas kernels for 0% -> 0%
where the time goes in v3:
time: 106 us
  waiting for transfers between devices  33.8 us (32%)
  local copies, waits for them, and re-layouts  14.8 us (14%)
  other arithmetic  14.7 us (14%)
  matrix products  14.2 us (13%)
  between operations  14.2 us (13%)
  starting transfers between devices  13.9 us (13%)
    reduce_scatter x1, waiting for transfers between devices, on_device(): lax.psum_scatter(((near_weight + far_weight) * (1.0 / data_groups)).astyp...  11.6 us
    ppermute x4, waiting for transfers between devices, seq_swap(): return lax.ppermute(x, 'seq', [(0, 1), (1, 0)])  11.1 us
    ppermute x3, waiting for transfers between devices, on_device(): lax.ppermute(summed, 'expert', [(jj, jj ^ k) for jj in range(experts)])  8.12 us
    ppermute x7, starting transfers between devices, on_device(): received[ds, k] = lax.ppermute(payload[k], ('seq', 'expert'), pairs(ds, k))  7.86 us
    gather x4, local copies, waits for them, and re-layouts, saved_rows(): return jnp.take(half, order, axis=0)  7.74 us
    dot_general x2, matrix products, expert_rows(): lax.dot_general(rows, w_out_half, (((1,), (1,)), ((), ())), preferred_ele...  4.5 us
    ppermute x4, starting transfers between devices, seq_swap(): return lax.ppermute(x, 'seq', [(0, 1), (1, 0)])  4.05 us
    dot_general x2, matrix products, expert_rows(): lax.dot_general(input_rows.reshape(count, model_width), delta_rows, (((0,...  4.03 us
  transfers between devices with their start and end apart: 15, of which 8 were waited for; matrix products, arithmetic and copies ran while one was open for 23% of the time, Pallas kernels for 0%

profile of v3, /device:TPU:0, one launch (start us, length us, event | category | flops | bytes accessed | tf_op | source)
XLA Modules:
  0.0 105.7 jit_solution(6226536378444241624)
XLA Ops:
  13.6 3.4 %collective-permute-start.6 = (bf16[80,1024]{1,0:T(8,128)(2,1)}, bf16[80,1024]{1,0:T(8,128)(2,1)}, u32[]{:S(2)}, u32[]{:S(2)}) collective-permute-start(bf16[80,1024]{1,0:T(8,128)(2,1)} %get-tuple-element.25), channel_id=1, source_target_pairs={{0,7},{1,6},{2,5},{3,4},{4,3},{5,2},{6,1},{7,0},{8,15},{9,14},{10,... | collective-permute-start | bytes 491528 | tf_op jit(solution)/shard_map/ppermute | solution.py:105
  19.3 2.0 %collective-permute-start.3 = (bf16[80,1024]{1,0:T(8,128)(2,1)}, bf16[80,1024]{1,0:T(8,128)(2,1)}, u32[]{:S(2)}, u32[]{:S(2)}) collective-permute-start(bf16[80,1024]{1,0:T(8,128)(2,1)} %get-tuple-element.24), channel_id=1, source_target_pairs={{0,4},{1,5},{2,6},{3,7},{4,0},{5,1},{6,2},{7,3},{8,12},{9,13},{10,... | collective-permute-start | bytes 491528 | tf_op jit(solution)/shard_map/ppermute | solution.py:105
  21.3 2.9 %dynamic-slice_bitcast_fusion = (bf16[4,72,1024]{2,1,0:T(8,128)(2,1)}, bf16[4,72,1024]{2,1,0:T(8,128)(2,1)}, bf16[4,72,1024]{2,1,0:T(8,128)(2,1)S(1)}, bf16[4,72,1024]{2,1,0:T(8,128)(2,1)S(1)}) fusion(bf16[1,1,4,2,72,1024]{5,4,3,2,1,0:T(8,128)(2,1)} %param.12, s32[]{:T(128)S(6)} %select_n.33, s32[]{:T(128)S(6)} %select_n.32, ...), kind=kLoop, calls=%fused_computation.52 | loop fusion | bytes 4718600 | tf_op jit(solution)/shard_map/jit(dynamic_index_in_dim)/squeeze | solution.py:113
  24.2 2.5 %gather_fusion.3 = bf16[4,72,1024]{2,1,0:T(8,128)(2,1)} fusion(bf16[4,72,1024]{2,1,0:T(8,128)(2,1)} %get-tuple-element.12, s32[1024]{0:T(1024)S(1)} %pad_clamp_fusion), kind=kCustom, calls=%fused_computation.3.clone | custom fusion | bytes 1179664 | tf_op jit(solution)/shard_map/jit(_take)/gather | solution.py:114
  26.6 2.5 %gather_fusion.2 = bf16[4,72,1024]{2,1,0:T(8,128)(2,1)} fusion(bf16[4,72,1024]{2,1,0:T(8,128)(2,1)} %get-tuple-element.13, s32[1024]{0:T(1024)S(1)} %pad_clamp_fusion), kind=kCustom, calls=%fused_computation.2.clone | custom fusion | bytes 1179664 | tf_op jit(solution)/shard_map/jit(_take)/gather | solution.py:114
  32.1 2.9 %broadcast_select_fusion = (bf16[4,72,1024]{2,1,0:T(8,128)(2,1)S(1)}, bf16[4,72,1024]{2,1,0:T(8,128)(2,1)}, bf16[4,72,1024]{2,1,0:T(8,128)(2,1)S(1)}, bf16[4,72,1024]{2,1,0:T(8,128)(2,1)}) fusion(bf16[4,72,1024]{2,1,0:T(8,128)(2,1)} %gather_fusion.3, pred[4]{0:T(512)(128)(4,1)S(1)} %compare_and_fusion, bf16[4,72,1024]{2,1,0:T(8,128)(2,1)} %gather_fusion.1, ...), kind=kLoop, calls=%fused_computation.56 | loop fusion | flops 1179648 | bytes 4718596 | tf_op jit(solution)/shard_map/jit(_take)/select_n | solution.py:114
  35.0 2.9 %collective-permute-done.4 = bf16[80,1024]{1,0:T(8,128)(2,1)S(1)} collective-permute-done((bf16[80,1024]{1,0:T(8,128)(2,1)}, bf16[80,1024]{1,0:T(8,128)(2,1)S(1)}, u32[]{:S(2)}, u32[]{:S(2)}) %collective-permute-start.4) | collective-permute-done | bytes 163872 | tf_op jit(solution)/shard_map/ppermute | solution.py:105
  38.6 1.9 %pad_maximum_fusion.1 = bf16[4,72,1024]{2,1,0:T(8,128)(2,1)} fusion(bf16[1,80,1024]{2,1,0:T(8,128)(2,1)} %bitcast.24, bf16[1,80,1024]{2,1,0:T(8,128)(2,1)} %bitcast.23, bf16[1,80,1024]{2,1,0:T(8,128)(2,1)S(1)} %bitcast.142, bf16[1,80,1024]{2,1,0:T(8,128)(2,1)} %bitcast.21), kind=kLoop, calls=%fused_computation.46 | loop fusion | flops 2359296 | bytes 1245184 | tf_op jit(solution)/shard_map/stack | solution.py:107
  41.2 1.9 %pad_maximum_fusion.4 = bf16[4,72,1024]{2,1,0:T(8,128)(2,1)} fusion(bf16[1,80,1024]{2,1,0:T(8,128)(2,1)} %bitcast.10, bf16[1,80,1024]{2,1,0:T(8,128)(2,1)} %bitcast.8, bf16[1,80,1024]{2,1,0:T(8,128)(2,1)S(1)} %bitcast.140, bf16[1,80,1024]{2,1,0:T(8,128)(2,1)S(1)} %get-tuple-element.28), kind=kLoop, calls=%fused_computation.49 | loop fusion | flops 2359296 | bytes 1245184 | tf_op jit(solution)/shard_map/stack | solution.py:106
  43.3 2.9 %fusion.16 = (bf16[288,1024]{1,0:T(8,128)(2,1)S(1)}, f32[288]{0:T(512)S(1)}) fusion(f32[288]{0:T(512)S(1)} %reshape.136, bf16[4,72,1024]{2,1,0:T(8,128)(2,1)} %get-tuple-element.32, bf16[288,1024]{1,0:T(8,128)(2,1)} %bitcast.151, bf16[288,1024]{1,0:T(8,128)(2,1)} %bitcast.154, bf16[1,1024,1024]{2,1,0:T(8,128)(2,1)S(1)} %copy-done), kind=kOutput, calls=%fused_computation.32 | convolution fusion | flops 609287936 | bytes 4458752 | tf_op jit(solution)/shard_map/dot_general | solution.py:43
  47.7 1.6 %fusion.25 = (bf16[288,1024]{1,0:T(8,128)(2,1)S(1)}, bf16[288]{0:T(512)(128)(2,1)S(1)}) fusion(f32[288]{0:T(512)S(1)} %reshape.138, bf16[4,72,1024]{2,1,0:T(8,128)(2,1)S(1)} %copy-done.3, bf16[288,1024]{1,0:T(8,128)(2,1)S(1)} %bitcast.150, bf16[288,1024]{1,0:T(8,128)(2,1)S(1)} %bitcast.153, bf16[1,1024,1024]{2,1,0:T(8,128)(2,1)S(1)} %copy-done), kind=kOutput, calls=%fused_computation.41 | convolution fusion | flops 609287936 | bytes 4458176 | tf_op jit(solution)/shard_map/dot_general | solution.py:43
  49.2 2.7 %multiply_convert_fusion = bf16[1024,1024]{1,0:T(8,128)(2,1)} fusion(f32[1024,1024]{1,0:T(8,128)S(1)} %fusion.51, bf16[288,1024]{1,0:T(8,128)(2,1)S(1)} %bitcast.136, bf16[288,1024]{1,0:T(8,128)(2,1)S(1)} %get-tuple-element.14), kind=kOutput, calls=%fused_computation.4 | convolution fusion | flops 607125504 | bytes 7471104 | tf_op jit(solution)/shard_map/dot_general | solution.py:59
  52.1 2.6 %fusion = bf16[4,72,1024]{2,1,0:T(8,128)(2,1)S(1)} fusion(bf16[4,72,1024]{2,1,0:T(8,128)(2,1)S(1)} %bitcast.152, bf16[1,1024,1024]{2,1,0:T(8,128)(2,1)} %param.14), kind=kOutput, calls=%fused_computation.5 | convolution fusion | flops 603979776 | bytes 3276800 | tf_op jit(solution)/shard_map/dot_general | solution.py:49
  55.8 1.8 %collective-permute-start.12 = (bf16[80,1024]{1,0:T(8,128)(2,1)}, bf16[80,1024]{1,0:T(8,128)(2,1)}, u32[]{:S(2)}, u32[]{:S(2)}) collective-permute-start(bf16[80,1024]{1,0:T(8,128)(2,1)} %get-tuple-element.21), channel_id=1, source_target_pairs={{0,4},{4,0},{1,5},{5,1},{2,6},{6,2},{3,7},{7,3},{8,12},{12,8},{9,1... | collective-permute-start | bytes 491528 | tf_op jit(solution)/shard_map/ppermute | solution.py:35
  57.8 1.8 %collective-permute-start.8 = (bf16[80,1024]{1,0:T(8,128)(2,1)}, bf16[80,1024]{1,0:T(8,128)(2,1)}, u32[]{:S(2)}, u32[]{:S(2)}) collective-permute-start(bf16[80,1024]{1,0:T(8,128)(2,1)} %get-tuple-element.23), channel_id=1, source_target_pairs={{0,4},{4,0},{1,5},{5,1},{2,6},{6,2},{3,7},{7,3},{8,12},{12,8},{9,1... | collective-permute-start | bytes 491528 | tf_op jit(solution)/shard_map/ppermute | solution.py:35
  60.7 2.1 %collective-permute-done.7 = bf16[80,1024]{1,0:T(8,128)(2,1)S(1)} collective-permute-done((bf16[80,1024]{1,0:T(8,128)(2,1)}, bf16[80,1024]{1,0:T(8,128)(2,1)S(1)}, u32[]{:S(2)}, u32[]{:S(2)}) %collective-permute-start.7) | collective-permute-done | bytes 163872 | tf_op jit(solution)/shard_map/ppermute | solution.py:35
  62.8 3.6 %collective-permute-done.12 = bf16[80,1024]{1,0:T(8,128)(2,1)} collective-permute-done((bf16[80,1024]{1,0:T(8,128)(2,1)}, bf16[80,1024]{1,0:T(8,128)(2,1)}, u32[]{:S(2)}, u32[]{:S(2)}) %collective-permute-start.12) | collective-permute-done | bytes 163872 | tf_op jit(solution)/shard_map/ppermute | solution.py:35
  66.4 3.5 %collective-permute-done.10 = bf16[80,1024]{1,0:T(8,128)(2,1)} collective-permute-done((bf16[80,1024]{1,0:T(8,128)(2,1)}, bf16[80,1024]{1,0:T(8,128)(2,1)}, u32[]{:S(2)}, u32[]{:S(2)}) %collective-permute-start.10) | collective-permute-done | bytes 163872 | tf_op jit(solution)/shard_map/ppermute | solution.py:35
  70.0 1.9 %collective-permute-done.8 = bf16[80,1024]{1,0:T(8,128)(2,1)} collective-permute-done((bf16[80,1024]{1,0:T(8,128)(2,1)}, bf16[80,1024]{1,0:T(8,128)(2,1)}, u32[]{:S(2)}, u32[]{:S(2)}) %collective-permute-start.8) | collective-permute-done | bytes 163872 | tf_op jit(solution)/shard_map/ppermute | solution.py:35
  73.3 1.7 %collective-permute-start.11 = (bf16[80,1024]{1,0:T(8,128)(2,1)S(1)}, bf16[80,1024]{1,0:T(8,128)(2,1)S(1)}, u32[]{:S(2)}, u32[]{:S(2)}) collective-permute-start(bf16[80,1024]{1,0:T(8,128)(2,1)S(1)} %get-tuple-element.10), channel_id=1, source_target_pairs={{0,2},{1,3},{2,0},{3,1},{4,6},{5,7},{6,4},{7,5},{8,10},{9,11},{10,... | collective-permute-start | bytes 491528 | tf_op jit(solution)/shard_map/ppermute | solution.py:138
  75.0 4.3 %collective-permute-done.13 = bf16[80,1024]{1,0:T(8,128)(2,1)S(1)} collective-permute-done((bf16[80,1024]{1,0:T(8,128)(2,1)S(1)}, bf16[80,1024]{1,0:T(8,128)(2,1)S(1)}, u32[]{:S(2)}, u32[]{:S(2)}) %collective-permute-start.13) | collective-permute-done | bytes 163872 | tf_op jit(solution)/shard_map/ppermute | solution.py:138
  79.3 3.8 %collective-permute-done.11 = bf16[80,1024]{1,0:T(8,128)(2,1)S(1)} collective-permute-done((bf16[80,1024]{1,0:T(8,128)(2,1)S(1)}, bf16[80,1024]{1,0:T(8,128)(2,1)S(1)}, u32[]{:S(2)}, u32[]{:S(2)}) %collective-permute-start.11) | collective-permute-done | bytes 163872 | tf_op jit(solution)/shard_map/ppermute | solution.py:138
  85.1 11.6 %reduce-scatter.2.cloned.1.call-done = bf16[256,1024]{1,0:T(8,128)(2,1)} async-done(((bf16[1024,1024]{1,0:T(8,128)(2,1)}), bf16[256,1024]{1,0:T(8,128)(2,1)}) %reduce-scatter.2.cloned.1.call-update) | async-done | bytes 524304 | tf_op jit(solution)/shard_map/reduce_scatter | solution.py:124
  96.7 2.1 %bitcast_convert_fusion = f32[1,256,1024]{2,1,0:T(8,128)} fusion(bf16[256,1024]{1,0:T(8,128)(2,1)} %reduce-scatter.2.cloned.1.call-done), kind=kLoop, calls=%fused_computation.60 | loop fusion | flops 262144 | bytes 1572864 | tf_op jit(solution)/shard_map/broadcast_in_dim | solution.py:130
  (76 shorter events, 20.8 us)
Async XLA Ops:
  7.2 36.1 %copy-start = (bf16[1,1024,1024]{2,1,0:T(8,128)(2,1)S(1)}, bf16[1,1024,1024]{2,1,0:T(8,128)(2,1)}, u32[]{:S(2)}) copy-start(bf16[1,1024,1024]{2,1,0:T(8,128)(2,1)} %param.15) | copy-start | bytes 6291460
  7.2 89.5 %reduce-scatter.2.cloned.1.call-start = ((), (), s32[]{:S(2)}) async-start(), calls=%async_computation.1 | async-start | bytes 2621440 | tf_op jit(solution)/shard_map/reduce_scatter | solution.py:124
  13.6 18.4 %collective-permute-start.6 = (bf16[80,1024]{1,0:T(8,128)(2,1)}, bf16[80,1024]{1,0:T(8,128)(2,1)}, u32[]{:S(2)}, u32[]{:S(2)}) collective-permute-start(bf16[80,1024]{1,0:T(8,128)(2,1)} %get-tuple-element.25), channel_id=1, source_target_pairs={{0,7},{1,6},{2,5},{3,4},{4,3},{5,2},{6,1},{7,0},{8,15},{9,14},{10,... | collective-permute-start | bytes 491528 | tf_op jit(solution)/shard_map/ppermute | solution.py:105
  17.0 23.5 %collective-permute-start.2 = (bf16[80,1024]{1,0:T(8,128)(2,1)}, bf16[80,1024]{1,0:T(8,128)(2,1)}, u32[]{:S(2)}, u32[]{:S(2)}) collective-permute-start(bf16[80,1024]{1,0:T(8,128)(2,1)} %get-tuple-element.25), channel_id=1, source_target_pairs={{0,3},{1,2},{2,1},{3,0},{4,7},{5,6},{6,5},{7,4},{8,11},{9,10},{10,... | collective-permute-start | bytes 491528 | tf_op jit(solution)/shard_map/ppermute | solution.py:105
  17.8 17.2 %collective-permute-start.5 = (bf16[80,1024]{1,0:T(8,128)(2,1)}, bf16[80,1024]{1,0:T(8,128)(2,1)}, u32[]{:S(2)}, u32[]{:S(2)}) collective-permute-start(bf16[80,1024]{1,0:T(8,128)(2,1)} %get-tuple-element.26), channel_id=1, source_target_pairs={{0,6},{1,7},{2,4},{3,5},{4,2},{5,3},{6,0},{7,1},{8,14},{9,15},{10,... | collective-permute-start | bytes 491528 | tf_op jit(solution)/shard_map/ppermute | solution.py:105
  19.2 21.3 %collective-permute-start.1 = (bf16[80,1024]{1,0:T(8,128)(2,1)}, bf16[80,1024]{1,0:T(8,128)(2,1)}, u32[]{:S(2)}, u32[]{:S(2)}) collective-permute-start(bf16[80,1024]{1,0:T(8,128)(2,1)} %get-tuple-element.26), channel_id=1, source_target_pairs={{0,2},{1,3},{2,0},{3,1},{4,6},{5,7},{6,4},{7,5},{8,10},{9,11},{10,... | collective-permute-start | bytes 491528 | tf_op jit(solution)/shard_map/ppermute | solution.py:105
  19.3 12.7 %collective-permute-start.3 = (bf16[80,1024]{1,0:T(8,128)(2,1)}, bf16[80,1024]{1,0:T(8,128)(2,1)}, u32[]{:S(2)}, u32[]{:S(2)}) collective-permute-start(bf16[80,1024]{1,0:T(8,128)(2,1)} %get-tuple-element.24), channel_id=1, source_target_pairs={{0,4},{1,5},{2,6},{3,7},{4,0},{5,1},{6,2},{7,3},{8,12},{9,13},{10,... | collective-permute-start | bytes 491528 | tf_op jit(solution)/shard_map/ppermute | solution.py:105
  31.9 6.0 %collective-permute-start.4 = (bf16[80,1024]{1,0:T(8,128)(2,1)}, bf16[80,1024]{1,0:T(8,128)(2,1)S(1)}, u32[]{:S(2)}, u32[]{:S(2)}) collective-permute-start(bf16[80,1024]{1,0:T(8,128)(2,1)} %get-tuple-element.27), channel_id=1, source_target_pairs={{0,5},{1,4},{2,7},{3,6},{4,1},{5,0},{6,3},{7,2},{8,13},{9,12},{10,... | collective-permute-start | bytes 491528 | tf_op jit(solution)/shard_map/ppermute | solution.py:105
  32.0 8.5 %collective-permute-start = (bf16[80,1024]{1,0:T(8,128)(2,1)}, bf16[80,1024]{1,0:T(8,128)(2,1)S(1)}, u32[]{:S(2)}, u32[]{:S(2)}) collective-permute-start(bf16[80,1024]{1,0:T(8,128)(2,1)} %get-tuple-element.27), channel_id=1, source_target_pairs={{0,1},{1,0},{2,3},{3,2},{4,5},{5,4},{6,7},{7,6},{8,9},{9,8},{10,11... | collective-permute-start | bytes 491528 | tf_op jit(solution)/shard_map/ppermute | solution.py:105
  46.2 1.3 %copy-start.1 = (bf16[288,1024]{1,0:T(8,128)(2,1)}, bf16[288,1024]{1,0:T(8,128)(2,1)S(1)}, u32[]{:S(2)}) copy-start(bf16[288,1024]{1,0:T(8,128)(2,1)S(1)} %get-tuple-element.18) | copy-start | bytes 1769476
  46.2 1.3 %copy-start.3 = (bf16[4,72,1024]{2,1,0:T(8,128)(2,1)S(1)}, bf16[4,72,1024]{2,1,0:T(8,128)(2,1)}, u32[]{:S(2)}) copy-start(bf16[4,72,1024]{2,1,0:T(8,128)(2,1)} %get-tuple-element.30) | copy-start | bytes 1769476
  46.2 1.4 %copy-start.4 = (bf16[4,72,1024]{2,1,0:T(8,128)(2,1)S(1)}, bf16[4,72,1024]{2,1,0:T(8,128)(2,1)}, u32[]{:S(2)}) copy-start(bf16[4,72,1024]{2,1,0:T(8,128)(2,1)} %pad_maximum_fusion.1) | copy-start | bytes 1769476
  52.1 7.5 %copy-start.5 = (bf16[1,1024,1024]{2,1,0:T(8,128)(2,1)S(1)}, bf16[1,1024,1024]{2,1,0:T(8,128)(2,1)}, u32[]{:S(2)}) copy-start(bf16[1,1024,1024]{2,1,0:T(8,128)(2,1)} %param.14) | copy-start | bytes 6291460
  54.6 5.0 %copy-start.2 = (bf16[288,1024]{1,0:T(8,128)(2,1)S(1)}, bf16[288,1024]{1,0:T(8,128)(2,1)}, u32[]{:S(2)}) copy-start(bf16[288,1024]{1,0:T(8,128)(2,1)} %copy-done.1) | copy-start | bytes 1769476
  55.5 7.3 %collective-permute-start.7 = (bf16[80,1024]{1,0:T(8,128)(2,1)}, bf16[80,1024]{1,0:T(8,128)(2,1)S(1)}, u32[]{:S(2)}, u32[]{:S(2)}) collective-permute-start(bf16[80,1024]{1,0:T(8,128)(2,1)} %get-tuple-element.20), channel_id=1, source_target_pairs={{0,4},{4,0},{1,5},{5,1},{2,6},{6,2},{3,7},{7,3},{8,12},{12,8},{9,1... | collective-permute-start | bytes 491528 | tf_op jit(solution)/shard_map/ppermute | solution.py:35
  55.8 10.6 %collective-permute-start.12 = (bf16[80,1024]{1,0:T(8,128)(2,1)}, bf16[80,1024]{1,0:T(8,128)(2,1)}, u32[]{:S(2)}, u32[]{:S(2)}) collective-permute-start(bf16[80,1024]{1,0:T(8,128)(2,1)} %get-tuple-element.21), channel_id=1, source_target_pairs={{0,4},{4,0},{1,5},{5,1},{2,6},{6,2},{3,7},{7,3},{8,12},{12,8},{9,1... | collective-permute-start | bytes 491528 | tf_op jit(solution)/shard_map/ppermute | solution.py:35
  57.6 12.4 %collective-permute-start.10 = (bf16[80,1024]{1,0:T(8,128)(2,1)}, bf16[80,1024]{1,0:T(8,128)(2,1)}, u32[]{:S(2)}, u32[]{:S(2)}) collective-permute-start(bf16[80,1024]{1,0:T(8,128)(2,1)} %get-tuple-element.22), channel_id=1, source_target_pairs={{0,4},{4,0},{1,5},{5,1},{2,6},{6,2},{3,7},{7,3},{8,12},{12,8},{9,1... | collective-permute-start | bytes 491528 | tf_op jit(solution)/shard_map/ppermute | solution.py:35
  57.8 14.0 %collective-permute-start.8 = (bf16[80,1024]{1,0:T(8,128)(2,1)}, bf16[80,1024]{1,0:T(8,128)(2,1)}, u32[]{:S(2)}, u32[]{:S(2)}) collective-permute-start(bf16[80,1024]{1,0:T(8,128)(2,1)} %get-tuple-element.23), channel_id=1, source_target_pairs={{0,4},{4,0},{1,5},{5,1},{2,6},{6,2},{3,7},{7,3},{8,12},{12,8},{9,1... | collective-permute-start | bytes 491528 | tf_op jit(solution)/shard_map/ppermute | solution.py:35
  73.1 6.2 %collective-permute-start.13 = (bf16[80,1024]{1,0:T(8,128)(2,1)S(1)}, bf16[80,1024]{1,0:T(8,128)(2,1)S(1)}, u32[]{:S(2)}, u32[]{:S(2)}) collective-permute-start(bf16[80,1024]{1,0:T(8,128)(2,1)S(1)} %get-tuple-element.9), channel_id=1, source_target_pairs={{0,3},{1,2},{2,1},{3,0},{4,7},{5,6},{6,5},{7,4},{8,11},{9,10},{10,... | collective-permute-start | bytes 491528 | tf_op jit(solution)/shard_map/ppermute | solution.py:138
  73.3 9.8 %collective-permute-start.11 = (bf16[80,1024]{1,0:T(8,128)(2,1)S(1)}, bf16[80,1024]{1,0:T(8,128)(2,1)S(1)}, u32[]{:S(2)}, u32[]{:S(2)}) collective-permute-start(bf16[80,1024]{1,0:T(8,128)(2,1)S(1)} %get-tuple-element.10), channel_id=1, source_target_pairs={{0,2},{1,3},{2,0},{3,1},{4,6},{5,7},{6,4},{7,5},{8,10},{9,11},{10,... | collective-permute-start | bytes 491528 | tf_op jit(solution)/shard_map/ppermute | solution.py:138
  75.0 8.2 %collective-permute-start.9 = (bf16[80,1024]{1,0:T(8,128)(2,1)S(1)}, bf16[80,1024]{1,0:T(8,128)(2,1)S(1)}, u32[]{:S(2)}, u32[]{:S(2)}) collective-permute-start(bf16[80,1024]{1,0:T(8,128)(2,1)S(1)} %get-tuple-element.11), channel_id=1, source_target_pairs={{0,1},{1,0},{2,3},{3,2},{4,5},{5,4},{6,7},{7,6},{8,9},{9,8},{10,11... | collective-permute-start | bytes 491528 | tf_op jit(solution)/shard_map/ppermute | solution.py:138
Sparse Core Ops, SparseCore 0:
  52.1 44.5 reduce-scatter.1
